TPU v7x, 32 devices: a whole 2x2x4 slice. The times are simulated.
32 devices in a mesh: dp: 16 (over z, x, core), head: 2 (over y).
Axes of the slice: x: 2, y: 2, z: 4, core: 2. Of those that a mesh axis runs over, the one named last changes fastest.
Arguments:
- inputs: float32 [512, 96, 512], P('dp', None, 'head'), may hold values from -6 to 6
- out_grad: float32 [512, 96, 512], P('dp', None, 'head'), may hold values from -6 to 6
- modes: int32 [8, 48], P('head'), may hold values from 0 to 48
- gates: int32 [2, 512, 96], P(None, 'dp'), may hold values from 0 to 4
- query_weight: float32 [512, 512], P(None, 'head'), may hold values from -0.25 to 0.25
- mixer_weight: float32 [8, 3072, 128], P('head'), may hold values from -0.42 to 0.42
- output_weight: float32 [512, 512], P('head'), may hold values from -0.25 to 0.25
- inner_weight: float32 [512, 2048], P(None, 'head'), may hold values from -0.25 to 0.25
- outer_weight: float32 [2048, 512], P('head'), may hold values from -0.125 to 0.125
- query_momentum: float32 [512, 512], P('dp', 'head'), may hold values from -80 to 80
- query_average: float32 [512, 512], P('dp', 'head'), may hold values from -0.25 to 0.25
- mixer_momentum: float32 [8, 3072, 128], P('head', 'dp'), may hold values from -32 to 32
- mixer_average: float32 [8, 3072, 128], P('head', 'dp'), may hold values from -0.42 to 0.42
- output_momentum: float32 [512, 512], P('head', 'dp'), may hold values from -128 to 128
- output_average: float32 [512, 512], P('head', 'dp'), may hold values from -0.25 to 0.25
- inner_momentum: float32 [512, 2048], P('dp', 'head'), may hold values from -40 to 40
- inner_average: float32 [512, 2048], P('dp', 'head'), may hold values from -0.25 to 0.25
- outer_momentum: float32 [2048, 512], P('head', 'dp'), may hold values from -80 to 80
- outer_average: float32 [2048, 512], P('head', 'dp'), may hold values from -0.125 to 0.125
Outputs:
- output: float32 [512, 96, 512], P('dp', None, 'head')
- input_grad: float32 [512, 96, 512], P('dp', None, 'head')
- query_momentum_new: float32 [512, 512], P('dp', 'head')
- query_weight_new: float32 [512, 512], P('dp', 'head')
- query_average_new: float32 [512, 512], P('dp', 'head')
- mixer_momentum_new: float32 [8, 3072, 128], P('head', 'dp')
- mixer_weight_new: float32 [8, 3072, 128], P('head', 'dp')
- mixer_average_new: float32 [8, 3072, 128], P('head', 'dp')
- output_momentum_new: float32 [512, 512], P('head', 'dp')
- output_weight_new: float32 [512, 512], P('head', 'dp')
- output_average_new: float32 [512, 512], P('head', 'dp')
- inner_momentum_new: float32 [512, 2048], P('dp', 'head')
- inner_weight_new: float32 [512, 2048], P('dp', 'head')
- inner_average_new: float32 [512, 2048], P('dp', 'head')
- outer_momentum_new: float32 [2048, 512], P('head', 'dp')
- outer_weight_new: float32 [2048, 512], P('head', 'dp')
- outer_average_new: float32 [2048, 512], P('head', 'dp')
Inputs may be any that keep to these rules, and one draw needn't show every extreme that they name: `modes`: bins of the real transform of a 96-step window; a head may name a bin more than once. `gates`: number of the pool (sizes 7, 12, 14, 24, 48 in this order).
All inputs are finite; a program needn't handle non-finite values.
Results may differ from a plain program's by a relative error of at most 0.018.
Values may be sent and summed in bfloat16 or wider, within the bound.
No kernel may reach another device: no remote copies, remote signals or barrier semaphores. Data moves between devices by JAX's collectives and lax.ppermute only.
A program may use at most 192 MiB of HBM per device.

v0:
```python
import math

import jax
import jax.numpy as jnp
import numpy as np
from jax import lax
from jax.sharding import PartitionSpec as P

D = 512
FF = 2048


highest = lax.Precision.HIGHEST
pool_sizes = (7, 12, 14, 24, 48)
mixer_spread = 0.07
momentum_decay = 0.9
average_decay = 0.9


def pool_tables(length):
    tables = np.zeros((len(pool_sizes), length, length), np.float32)
    rows_all = np.arange(length)
    for pool_index, pool_width in enumerate(pool_sizes):
        lead_pad = (pool_width - 1) // 2
        for offset in range(pool_width):
            source = np.clip(rows_all - lead_pad + offset, 0, length - 1)
            tables[pool_index][rows_all, source] += np.float32(1.0 / pool_width)
    return jnp.asarray(tables)


def spectral_tables(modes, length):
    positions = jnp.arange(length, dtype=jnp.int32)
    phase = modes[:, :, None] * positions[None, None, :] % length
    angle = phase.astype(jnp.float32) * (2.0 * math.pi / length)
    cosine = jnp.cos(angle)
    sine = jnp.sin(angle)
    doubled = jnp.where((modes == 0) | (2 * modes == length), 1.0, 2.0).astype(jnp.float32) / length
    inv_cos = jnp.transpose(doubled[:, :, None] * cosine, (0, 2, 1))
    inv_sin = jnp.transpose(-doubled[:, :, None] * sine, (0, 2, 1))
    return (cosine, -sine, inv_cos, inv_sin)


def product(form, left, right):
    return jnp.einsum(form, left, right, preferred_element_type=jnp.float32)


def trend_local(values, picks, pools):
    total = jnp.zeros_like(values)
    for pool_index in range(len(pool_sizes)):
        chosen = (picks == pool_index).astype(jnp.float32)[..., None]
        total = total + chosen * jnp.einsum(
            "ts,wsd->wtd", pools[pool_index], values, precision=highest
        )
    return total


def trend_back(grads, picks, pools):
    total = jnp.zeros_like(grads)
    for pool_index in range(len(pool_sizes)):
        chosen = (picks == pool_index).astype(jnp.float32)[..., None]
        total = total + jnp.einsum(
            "ts,wtd->wsd", pools[pool_index], chosen * grads, precision=highest
        )
    return total


def mixer_block(mixer_low, head_size):
    head_count = mixer_low.shape[0]
    shaped = mixer_low.reshape(head_count, -1, head_size, 2 * head_size)
    real_part = shaped[..., :head_size]
    imag_part = shaped[..., head_size:]
    upper = jnp.concatenate([real_part, imag_part], axis=-1)
    lower = jnp.concatenate([-imag_part, real_part], axis=-1)
    return jnp.concatenate([upper, lower], axis=2)


def exact_gelu(values):
    return jax.nn.gelu(values, approximate=False)


def on_device(
    inputs,
    out_grad,
    modes,
    gates,
    query_weight,
    mixer_weight,
    output_weight,
    inner_weight,
    outer_weight,
    query_momentum,
    query_average,
    mixer_momentum,
    mixer_average,
    output_momentum,
    output_average,
    inner_momentum,
    inner_average,
    outer_momentum,
    outer_average,
):
    windows, length, local_width = inputs.shape
    head_count, mode_count = modes.shape
    head_size = local_width // head_count
    pools = pool_tables(length)
    fwd_cos, fwd_sin, inv_cos, inv_sin = [
        one_table.astype(jnp.bfloat16) for one_table in spectral_tables(modes, length)
    ]
    query_low = query_weight.astype(jnp.bfloat16)
    output_low = output_weight.astype(jnp.bfloat16)
    inner_low = inner_weight.astype(jnp.bfloat16)
    outer_low = outer_weight.astype(jnp.bfloat16)
    block = mixer_block(mixer_weight.astype(jnp.bfloat16), head_size)
    inputs_full = lax.all_gather(inputs.astype(jnp.bfloat16), "head", axis=2, tiled=True)
    query = product("wtd,de->wte", inputs_full, query_low).astype(jnp.bfloat16)
    query_heads = query.reshape(windows, length, head_count, head_size)
    spectrum = jnp.concatenate(
        [
            product("hmt,wthe->whme", fwd_cos, query_heads),
            product("hmt,wthe->whme", fwd_sin, query_heads),
        ],
        axis=-1,
    ).astype(jnp.bfloat16)
    mixed = product("whmi,hmio->whmo", spectrum, block).astype(jnp.bfloat16)
    field = product("htm,whme->wthe", inv_cos, mixed[..., :head_size]) + product(
        "htm,whme->wthe", inv_sin, mixed[..., head_size:]
    )
    field = field.reshape(windows, length, local_width).astype(jnp.bfloat16)
    attended = lax.psum_scatter(
        product("wte,ed->wtd", field, output_low).astype(jnp.bfloat16),
        "head",
        scatter_dimension=2,
        tiled=True,
    ).astype(jnp.float32)
    resid_one = inputs + attended
    seasonal = resid_one - trend_local(resid_one, gates[0], pools)
    seasonal_full = lax.all_gather(seasonal.astype(jnp.bfloat16), "head", axis=2, tiled=True)
    pre = product("wtd,df->wtf", seasonal_full, inner_low)
    activated, gelu_pull = jax.vjp(exact_gelu, pre)
    hidden = activated.astype(jnp.bfloat16)
    feed = lax.psum_scatter(
        product("wtf,fd->wtd", hidden, outer_low).astype(jnp.bfloat16),
        "head",
        scatter_dimension=2,
        tiled=True,
    ).astype(jnp.float32)
    combined = seasonal + feed
    output = combined - trend_local(combined, gates[1], pools)
    grad_comb = out_grad - trend_back(out_grad, gates[1], pools)
    grad_feed = lax.all_gather(grad_comb.astype(jnp.bfloat16), "head", axis=2, tiled=True)
    outer_grad = product("wtf,wtd->fd", hidden, grad_feed)
    grad_hidden = product("wtd,fd->wtf", grad_feed, outer_low)
    grad_pre = gelu_pull(grad_hidden)[0].astype(jnp.bfloat16)
    inner_grad = product("wtd,wtf->df", seasonal_full, grad_pre)
    grad_season = grad_comb + lax.psum_scatter(
        product("wtf,df->wtd", grad_pre, inner_low).astype(jnp.bfloat16),
        "head",
        scatter_dimension=2,
        tiled=True,
    ).astype(jnp.float32)
    grad_resid = grad_season - trend_back(grad_season, gates[0], pools)
    grad_attend = lax.all_gather(grad_resid.astype(jnp.bfloat16), "head", axis=2, tiled=True)
    output_grad = product("wte,wtd->ed", field, grad_attend)
    grad_field = product("wtd,ed->wte", grad_attend, output_low).astype(jnp.bfloat16)
    grad_field = grad_field.reshape(windows, length, head_count, head_size)
    grad_mixed = jnp.concatenate(
        [
            product("htm,wthe->whme", inv_cos, grad_field),
            product("htm,wthe->whme", inv_sin, grad_field),
        ],
        axis=-1,
    ).astype(jnp.bfloat16)
    grad_spectrum = product("whmo,hmio->whmi", grad_mixed, block).astype(jnp.bfloat16)
    grad_query = product("hmt,whme->wthe", fwd_cos, grad_spectrum[..., :head_size]) + product(
        "hmt,whme->wthe", fwd_sin, grad_spectrum[..., head_size:]
    )
    grad_query = grad_query.reshape(windows, length, local_width).astype(jnp.bfloat16)
    query_grad = product("wtd,wte->de", inputs_full, grad_query)
    input_grad = grad_resid + lax.psum_scatter(
        product("wte,de->wtd", grad_query, query_low).astype(jnp.bfloat16),
        "head",
        scatter_dimension=2,
        tiled=True,
    ).astype(jnp.float32)
    query_part, inner_part = (
        lax.psum_scatter(query_grad, "dp", scatter_dimension=0, tiled=True),
        lax.psum_scatter(inner_grad, "dp", scatter_dimension=0, tiled=True),
    )
    block_grad = product("whmi,whmo->hmio", spectrum, grad_mixed)
    real_grad = block_grad[:, :, :head_size, :head_size] + block_grad[:, :, head_size:, head_size:]
    imag_grad = block_grad[:, :, :head_size, head_size:] - block_grad[:, :, head_size:, :head_size]
    mixer_full = jnp.concatenate([real_grad, imag_grad], axis=-1).reshape(
        head_count, mode_count * head_size, 2 * head_size
    )
    mixer_part, output_part, outer_part = (
        lax.psum_scatter(mixer_full, "dp", scatter_dimension=1, tiled=True),
        lax.psum_scatter(output_grad, "dp", scatter_dimension=1, tiled=True),
        lax.psum_scatter(outer_grad, "dp", scatter_dimension=1, tiled=True),
    )
    dp_count = lax.axis_size("dp")
    dp_rank = lax.axis_index("dp")
    token_total = windows * length * dp_count

    def owned(weight, share, axis_number):
        return lax.dynamic_slice_in_dim(weight, dp_rank * share, share, axis_number)

    def stepped(grad, momentum, average, old_weight, spread):
        rate = 0.5 * spread / math.sqrt(token_total)
        new_momentum = momentum_decay * momentum + grad
        new_weight = old_weight - rate * (grad + momentum_decay * new_momentum)
        new_average = average_decay * average + (1 - average_decay) * new_weight
        return (new_momentum, new_weight, new_average)

    query_new = stepped(
        query_part,
        query_momentum,
        query_average,
        owned(query_weight, query_momentum.shape[0], 0),
        D ** (-0.5),
    )
    mixer_new = stepped(
        mixer_part,
        mixer_momentum,
        mixer_average,
        owned(mixer_weight, mixer_momentum.shape[1], 1),
        mixer_spread,
    )
    output_new = stepped(
        output_part,
        output_momentum,
        output_average,
        owned(output_weight, output_momentum.shape[1], 1),
        D ** (-0.5),
    )
    inner_new = stepped(
        inner_part,
        inner_momentum,
        inner_average,
        owned(inner_weight, inner_momentum.shape[0], 0),
        D ** (-0.5),
    )
    outer_new = stepped(
        outer_part,
        outer_momentum,
        outer_average,
        owned(outer_weight, outer_momentum.shape[1], 1),
        FF ** (-0.5),
    )
    return (
        output,
        input_grad,
        query_new[0],
        query_new[1],
        query_new[2],
        mixer_new[0],
        mixer_new[1],
        mixer_new[2],
        output_new[0],
        output_new[1],
        output_new[2],
        inner_new[0],
        inner_new[1],
        inner_new[2],
        outer_new[0],
        outer_new[1],
        outer_new[2],
    )


def solution(mesh):
    return jax.shard_map(
        on_device,
        mesh=mesh,
        in_specs=(
            P("dp", None, "head"),
            P("dp", None, "head"),
            P("head", None),
            P(None, "dp", None),
            P(None, "head"),
            P("head", None, None),
            P("head", None),
            P(None, "head"),
            P("head", None),
            P("dp", "head"),
            P("dp", "head"),
            P("head", "dp", None),
            P("head", "dp", None),
            P("head", "dp"),
            P("head", "dp"),
            P("dp", "head"),
            P("dp", "head"),
            P("head", "dp"),
            P("head", "dp"),
        ),
        out_specs=(
            P("dp", None, "head"),
            P("dp", None, "head"),
            P("dp", "head"),
            P("dp", "head"),
            P("dp", "head"),
            P("head", "dp", None),
            P("head", "dp", None),
            P("head", "dp", None),
            P("head", "dp"),
            P("head", "dp"),
            P("head", "dp"),
            P("dp", "head"),
            P("dp", "head"),
            P("dp", "head"),
            P("head", "dp"),
            P("head", "dp"),
            P("head", "dp"),
        ),
        check_vma=False,
    )
```

profile of v0, /device:TPU:0, one launch (start us, length us, event | category | flops | bytes accessed | tf_op | source)
XLA Modules:
  0.0 811.5 jit_solution(15718903586019919572)
XLA Ops:
  7.2 3.3 convert_element_type.225
  10.6 3.2 convert_element_type.224
  13.8 4.0 slice_negate_fusion
  17.8 40.5 %all-gather.5.cloned.1.call-done = bf16[32,96,512]{2,1,0:T(8,128)(2,1)} async-done(((bf16[32,96,256]{2,1,0:T(8,128)(2,1)}), bf16[32,96,512]{2,1,0:T(8,128)(2,1)}) %all-gather.5.cloned.1.call-update) | async-done | bytes 3145744 | tf_op jit(solution)/shard_map/all_gather | solution.py:114
  58.3 4.1 convolution_convert_fusion.7
  62.4 4.4 copy.143
  66.8 3.9 fusion.76
  70.8 2.2 fusion.79
  75.0 3.1 fusion.69
  83.2 2.6 convolution_convert_fusion.3
  86.8 42.7 %reduce-scatter.12.cloned.1.call-done = bf16[32,96,256]{2,1,0:T(8,128)(2,1)} async-done(((bf16[32,96,512]{2,1,0:T(8,128)(2,1)}), bf16[32,96,256]{2,1,0:T(8,128)(2,1)}) %reduce-scatter.12.cloned.1.call-update) | async-done | bytes 1572880 | tf_op jit(solution)/shard_map/reduce_scatter | solution.py:129
  129.5 4.8 fusion.158
  134.3 3.3 fusion.157
  137.6 3.3 fusion.156
  141.0 3.7 fusion.159
  144.7 6.6 fusion.167
  151.4 5.4 fusion.24
  156.8 3.4 fusion.22
  160.2 3.4 fusion.18
  163.6 3.6 fusion.16
  167.2 5.5 fusion.168
  172.7 23.7 %all-gather.7.cloned.1.call-done = bf16[32,96,512]{2,1,0:T(8,128)(2,1)} async-done(((bf16[32,96,256]{2,1,0:T(8,128)(2,1)}), bf16[32,96,512]{2,1,0:T(8,128)(2,1)}) %all-gather.7.cloned.1.call-update) | async-done | bytes 3145744 | tf_op jit(solution)/shard_map/all_gather | solution.py:137
  196.4 8.3 %convert_reduce_fusion.1 = (u32[96,1024]{1,0:T(8,128)S(1)}, u32[96,1024]{1,0:T(8,128)S(1)}, f32[32,96,1024]{2,1,0:T(8,128)S(1)}) fusion(bf16[32,96,512]{2,1,0:T(8,128)(2,1)} %all-gather.7.cloned.1.call-done, f32[512,1024]{1,0:T(8,128)} %param.27), kind=kOutput, calls=%fused_computation.6 | convolution fusion | flops 3256156160 | bytes 18612224 | tf_op jit(solution)/shard_map/wtd,df->wtf/dot_general | solution.py:44
  204.7 4.8 copy-done.9
  209.6 29.0 %multiply_convert_fusion = (bf16[32,96,1024]{2,1,0:T(8,128)(2,1)}, f32[32,96,1024]{2,1,0:T(8,128)}) fusion(f32[32,96,1024]{2,1,0:T(8,128)S(1)} %get-tuple-element.109, u32[96,1024]{1,0:T(8,128)S(1)} %get-tuple-element.69, u32[96,1024]{1,0:T(8,128)S(1)} %get-tuple-element.68), kind=kLoop, calls=%fused_computation.8 | loop fusion | flops 213909504 | bytes 32243712 | tf_op jit(solution)/shard_map/convert_element_type | solution.py:140
  238.6 4.1 all-gather.9.cloned.1.call-done
  242.7 15.1 %add_convert_fusion = bf16[32,96,1024]{2,1,0:T(8,128)(2,1)} fusion(f32[32,96,1024]{2,1,0:T(8,128)} %get-tuple-element.86, f32[32,96,1024]{2,1,0:T(8,128)} %copy-done.9, bf16[32,96,512]{2,1,0:T(8,128)(2,1)} %all-gather.9.cloned.1.call-done, f32[1024,512]{1,0:T(8,128)} %param.28), kind=kOutput, calls=%fused_computation.7 | convolution fusion | flops 3265789952 | bytes 36700160 | tf_op jit(solution)/shard_map/wtd,fd->wtf/dot_general | solution.py:44
  257.8 7.7 convolution_convert_fusion.1
  266.0 43.1 %reduce-scatter.16.cloned.1.call-done = bf16[32,96,256]{2,1,0:T(8,128)(2,1)} async-done(((bf16[32,96,512]{2,1,0:T(8,128)(2,1)}), bf16[32,96,256]{2,1,0:T(8,128)(2,1)}) %reduce-scatter.16.cloned.1.call-update) | async-done | bytes 1572880 | tf_op jit(solution)/shard_map/reduce_scatter | solution.py:155
  309.1 4.9 fusion.12
  314.0 3.3 fusion.8
  317.3 3.3 fusion.6
  320.7 3.5 fusion.14
  324.2 5.9 fusion.169
  330.3 8.7 %convolution_bitcast_fusion.1 = f32[512,1024]{1,0:T(8,128)} fusion(bf16[32,96,512]{2,1,0:T(8,128)(2,1)} %all-gather.7.cloned.1.call-done, bf16[32,96,1024]{2,1,0:T(8,128)(2,1)} %add_convert_fusion), kind=kOutput, calls=%fused_computation.79 | convolution fusion | flops 3221225472 | bytes 11534336 | tf_op jit(solution)/shard_map/wtd,wtf->df/dot_general | solution.py:44
  339.0 8.8 %convolution_bitcast_fusion = f32[1024,512]{0,1:T(8,128)} fusion(bf16[32,96,1024]{2,1,0:T(8,128)(2,1)} %get-tuple-element.85, bf16[32,96,512]{2,1,0:T(8,128)(2,1)} %all-gather.9.cloned.1.call-done), kind=kOutput, calls=%fused_computation.78 | convolution fusion | flops 3221225472 | bytes 11534336 | tf_op jit(solution)/shard_map/wtf,wtd->fd/dot_general | solution.py:44
  347.9 7.7 convolution_convert_fusion.2
  355.7 19.6 %all-gather.11.cloned.1.call-done = bf16[32,96,512]{2,1,0:T(8,128)(2,1)} async-done(((bf16[32,96,256]{2,1,0:T(8,128)(2,1)}), bf16[32,96,512]{2,1,0:T(8,128)(2,1)}) %all-gather.11.cloned.1.call-update) | async-done | bytes 3145744 | tf_op jit(solution)/shard_map/all_gather | solution.py:162
  375.2 4.1 convolution_convert_fusion.6
  379.3 3.5 copy.161
  382.8 2.2 fusion.70
  385.0 2.2 fusion.73
  387.2 2.0 pad_maximum_fusion.2
  389.5 8.1 fusion.68
  397.5 2.6 fusion.165
  408.0 4.4 convolution_bitcast_fusion.2
  412.5 4.9 convolution_convert_fusion
  419.3 5.2 slice_add_fusion
  424.5 7.1 pad_maximum_fusion
  433.5 2.0 constant_dynamic-slice_fusion
  436.7 4.1 reduce-scatter.24.cloned.1.call-done
  442.7 62.6 %reduce-scatter.26.cloned.1.call-done = f32[1024,32]{0,1:T(8,128)} async-done(((f32[1024,512]{0,1:T(8,128)}), f32[1024,32]{0,1:T(8,128)}) %reduce-scatter.26.cloned.1.call-update) | async-done | bytes 131088 | tf_op jit(solution)/shard_map/reduce_scatter | solution.py:198
  507.1 42.8 %reduce-scatter.14.cloned.1.call-done = bf16[32,96,256]{2,1,0:T(8,128)(2,1)} async-done(((bf16[32,96,512]{2,1,0:T(8,128)(2,1)}), bf16[32,96,256]{2,1,0:T(8,128)(2,1)}) %reduce-scatter.14.cloned.1.call-update) | async-done | bytes 1572880 | tf_op jit(solution)/shard_map/reduce_scatter | solution.py:141
  550.0 4.7 fusion.162
  554.6 3.2 fusion.161
  557.8 3.2 fusion.160
  561.0 3.4 fusion.163
  564.4 6.0 bitcast_subtract_fusion.2
  570.4 39.1 %reduce-scatter.28.cloned.1.call-done = f32[32,256]{1,0:T(8,128)} async-done(((f32[512,256]{1,0:T(8,128)}), f32[32,256]{1,0:T(8,128)}) %reduce-scatter.28.cloned.1.call-update) | async-done | bytes 32784 | tf_op jit(solution)/shard_map/reduce_scatter | solution.py:186
  611.0 57.4 %reduce-scatter.22.cloned.1.call-done = f32[256,32]{0,1:T(8,128)} async-done(((f32[256,512]{0,1:T(8,128)}), f32[256,32]{0,1:T(8,128)}) %reduce-scatter.22.cloned.1.call-update) | async-done | bytes 32784 | tf_op jit(solution)/shard_map/reduce_scatter | solution.py:197
  669.8 43.8 %reduce-scatter.18.cloned.1.call-done = bf16[32,96,256]{2,1,0:T(8,128)(2,1)} async-done(((bf16[32,96,512]{2,1,0:T(8,128)(2,1)}), bf16[32,96,256]{2,1,0:T(8,128)(2,1)}) %reduce-scatter.18.cloned.1.call-update) | async-done | bytes 1572880 | tf_op jit(solution)/shard_map/reduce_scatter | solution.py:179
  713.5 4.7 convert_add_fusion
  718.2 84.4 %reduce-scatter.20.cloned.1.call-done = f32[4,192,128]{2,1,0:T(8,128)} async-done(((f32[4,3072,128]{2,1,0:T(8,128)}), f32[4,192,128]{2,1,0:T(8,128)}) %reduce-scatter.20.cloned.1.call-update) | async-done | bytes 393232 | tf_op jit(solution)/shard_map/reduce_scatter | solution.py:196
  802.6 2.2 multiply_add_fusion
  (135 shorter events, 28.6 us)
Async XLA Ops:
  7.2 51.1 %all-gather.5.cloned.1.call-start = ((), (), s32[]{:S(2)}) async-start(), calls=%async_computation.9 | async-start | bytes 4718592 | tf_op jit(solution)/shard_map/all_gather | solution.py:114
  10.5 3.3 copy-start.28
  10.6 118.9 %reduce-scatter.12.cloned.1.call-start = ((), (), s32[]{:S(2)}) async-start(), calls=%async_computation.10 | async-start | bytes 4718592 | tf_op jit(solution)/shard_map/reduce_scatter | solution.py:129
  13.8 60.0 %copy-start.6 = (bf16[4,3072,128]{2,1,0:T(8,128)(2,1)}, bf16[4,3072,128]{2,1,0:T(8,128)(2,1)S(1)}, u32[]{:S(2)}) copy-start(bf16[4,3072,128]{2,1,0:T(8,128)(2,1)S(1)} %convert_element_type.224) | copy-start | bytes 9437188
  66.8 4.0 copy-start.8
  70.7 3.1 copy-start.18
  73.0 2.0 copy-start.17
  73.9 4.2 copy-start.10
  81.7 1.5 copy-start.19
  81.9 1.3 copy-start.13
  83.2 2.9 copy-start.43
  83.2 46.3 %copy-start = (f32[32,96,256]{2,1,0:T(8,128)S(1)}, f32[32,96,256]{2,1,0:T(8,128)}, u32[]{:S(2)}) copy-start(f32[32,96,256]{2,1,0:T(8,128)} %param.20) | copy-start | bytes 9437188
  83.2 46.3 %copy-start.21 = (f32[96,96,1]{1,0,2:T(8,128)S(1)}, f32[96,96,1]{1,0,2:T(8,128)}, u32[]{:S(2)}) copy-start(f32[96,96,1]{1,0,2:T(8,128)} %constant.142) | copy-start | bytes 110596
  85.9 110.5 %all-gather.7.cloned.1.call-start = ((), (), s32[]{:S(2)}) async-start(), calls=%async_computation.11 | async-start | bytes 4718592 | tf_op jit(solution)/shard_map/all_gather | solution.py:137
  86.7 64.7 %copy-start.29 = (f32[32,96]{1,0:T(8,128)}, f32[32,96]{1,0:T(8,128)S(1)}, u32[]{:S(2)}) copy-start(f32[32,96]{1,0:T(8,128)S(1)} %get-tuple-element.95) | copy-start | bytes 36868
  86.7 70.1 %copy-start.31 = (f32[32,96]{1,0:T(8,128)}, f32[32,96]{1,0:T(8,128)S(1)}, u32[]{:S(2)}) copy-start(f32[32,96]{1,0:T(8,128)S(1)} %get-tuple-element.100) | copy-start | bytes 36868
  86.7 76.9 %copy-start.33 = (f32[32,96]{1,0:T(8,128)}, f32[32,96]{1,0:T(8,128)S(1)}, u32[]{:S(2)}) copy-start(f32[32,96]{1,0:T(8,128)S(1)} %get-tuple-element.103) | copy-start | bytes 36868
  86.7 47.5 %copy-start.25 = (f32[96,96,1]{1,0,2:T(8,128)S(1)}, f32[96,96,1]{1,0,2:T(8,128)}, u32[]{:S(2)}) copy-start(f32[96,96,1]{1,0,2:T(8,128)} %constant.143) | copy-start | bytes 110596
  129.5 4.8 copy-start.4
  134.3 3.3 copy-start.23
  137.6 3.3 copy-start.22
  141.0 3.7 copy-start.24
  141.0 3.7 copy-start.35
  151.4 91.3 %all-gather.9.cloned.1.call-start = ((), (), s32[]{:S(2)}) async-start(), calls=%async_computation.13 | async-start | bytes 4718592 | tf_op jit(solution)/shard_map/all_gather | solution.py:150
  151.4 5.4 copy-start.2
  172.7 136.4 %reduce-scatter.16.cloned.1.call-start = ((), (), s32[]{:S(2)}) async-start(), calls=%async_computation.14 | async-start | bytes 4718592 | tf_op jit(solution)/shard_map/reduce_scatter | solution.py:155
  204.7 4.8 copy-start.9
  242.7 15.1 %copy-start.44 = (f32[512,1024]{1,0:T(8,128)S(1)}, f32[512,1024]{1,0:T(8,128)}, u32[]{:S(2)}) copy-start(f32[512,1024]{1,0:T(8,128)} %param.27) | copy-start | bytes 6291460
  265.5 109.7 %all-gather.11.cloned.1.call-start = ((), (), s32[]{:S(2)}) async-start(), calls=%async_computation.15 | async-start | bytes 4718592 | tf_op jit(solution)/shard_map/all_gather | solution.py:162
  309.1 4.9 copy-start.5
  320.7 3.6 copy-start.36
  330.2 110.6 %reduce-scatter.24.cloned.1.call-start = ((), (), s32[]{:S(2)}) async-start(), calls=%async_computation.19 | async-start | bytes 2228224 | tf_op jit(solution)/shard_map/reduce_scatter | solution.py:187
  339.0 166.3 %reduce-scatter.26.cloned.1.call-start = ((), (), s32[]{:S(2)}) async-start(), calls=%async_computation.20 | async-start | bytes 2228224 | tf_op jit(solution)/shard_map/reduce_scatter | solution.py:198
  339.0 8.9 %copy-start.38 = (f32[1024,512]{1,0:T(8,128)S(1)}, f32[1024,512]{1,0:T(8,128)}, u32[]{:S(2)}) copy-start(f32[1024,512]{1,0:T(8,128)} %param.28) | copy-start | bytes 6291460
  347.9 202.1 %reduce-scatter.14.cloned.1.call-start = ((), (), s32[]{:S(2)}) async-start(), calls=%async_computation.12 | async-start | bytes 4718592 | tf_op jit(solution)/shard_map/reduce_scatter | solution.py:141
  355.6 19.6 %copy-start.20 = (f32[256,512]{1,0:T(8,128)S(1)}, f32[256,512]{1,0:T(8,128)}, u32[]{:S(2)}) copy-start(f32[256,512]{1,0:T(8,128)} %param.26) | copy-start | bytes 1572868
  355.6 253.9 %reduce-scatter.28.cloned.1.call-start = ((), (), s32[]{:S(2)}) async-start(), calls=%async_computation.21 | async-start | bytes 557056 | tf_op jit(solution)/shard_map/reduce_scatter | solution.py:186
  387.2 2.3 copy-start.7
  403.0 2.6 copy-start.16
  403.2 1.3 copy-start.15
  405.7 2.3 copy-start.14
  407.7 260.6 %reduce-scatter.22.cloned.1.call-start = ((), (), s32[]{:S(2)}) async-start(), calls=%async_computation.18 | async-start | bytes 557056 | tf_op jit(solution)/shard_map/reduce_scatter | solution.py:197
  412.4 5.0 copy-start.11
  412.4 5.0 copy-start.12
  412.4 301.1 %reduce-scatter.18.cloned.1.call-start = ((), (), s32[]{:S(2)}) async-start(), calls=%async_computation.16 | async-start | bytes 4718592 | tf_op jit(solution)/shard_map/reduce_scatter | solution.py:179
  417.4 385.2 %reduce-scatter.20.cloned.1.call-start = ((), (), s32[]{:S(2)}) async-start(), calls=%async_computation.17 | async-start | bytes 6684672 | tf_op jit(solution)/shard_map/reduce_scatter | solution.py:196
  431.6 118.4 %copy-start.1 = (f32[32,96,256]{2,1,0:T(8,128)S(1)}, f32[32,96,256]{2,1,0:T(8,128)}, u32[]{:S(2)}) copy-start(f32[32,96,256]{2,1,0:T(8,128)} %get-tuple-element.108) | copy-start | bytes 9437188
  550.0 4.7 copy-start.3
  561.0 3.4 copy-start.30
  561.0 3.4 copy-start.32
  561.0 3.4 copy-start.34
  564.4 45.2 %copy-start.39 = (f32[32,256]{1,0:T(8,128)S(1)}, f32[32,256]{1,0:T(8,128)}, u32[]{:S(2)}) copy-start(f32[32,256]{1,0:T(8,128)} %param.30) | copy-start | bytes 98308
  564.4 45.1 %copy-start.40 = (f32[32,256]{1,0:T(8,128)S(1)}, f32[32,256]{1,0:T(8,128)}, u32[]{:S(2)}) copy-start(f32[32,256]{1,0:T(8,128)} %param.29) | copy-start | bytes 98308
  564.4 103.9 %copy-start.37 = (f32[256,32]{0,1:T(8,128)S(1)}, f32[256,32]{0,1:T(8,128)}, u32[]{:S(2)}) copy-start(f32[256,32]{0,1:T(8,128)} %copy.207) | copy-start | bytes 98308
  564.4 103.9 %copy-start.41 = (f32[256,32]{0,1:T(8,128)S(1)}, f32[256,32]{0,1:T(8,128)}, u32[]{:S(2)}) copy-start(f32[256,32]{0,1:T(8,128)} %param.34) | copy-start | bytes 98308
  564.4 103.9 %copy-start.42 = (f32[256,32]{0,1:T(8,128)S(1)}, f32[256,32]{0,1:T(8,128)}, u32[]{:S(2)}) copy-start(f32[256,32]{0,1:T(8,128)} %param.33) | copy-start | bytes 98308
  713.5 89.0 %copy-start.26 = (f32[4,192,128]{2,1,0:T(8,128)S(1)}, f32[4,192,128]{2,1,0:T(8,128)}, u32[]{:S(2)}) copy-start(f32[4,192,128]{2,1,0:T(8,128)} %param.32) | copy-start | bytes 1179652
  713.5 89.0 %copy-start.27 = (f32[4,192,128]{2,1,0:T(8,128)S(1)}, f32[4,192,128]{2,1,0:T(8,128)}, u32[]{:S(2)}) copy-start(f32[4,192,128]{2,1,0:T(8,128)} %param.31) | copy-start | bytes 1179652
Sparse Core Ops, SparseCore 0:
  10.7 47.5 all-gather.4
  86.0 43.4 reduce-scatter.11
  151.5 44.8 all-gather.6
  197.8 44.8 all-gather.8
  265.6 43.3 reduce-scatter.15
  330.3 44.8 all-gather.10
  379.0 61.8 reduce-scatter.23
  444.6 60.6 reduce-scatter.25
  507.5 42.3 reduce-scatter.13
  553.3 56.1 reduce-scatter.27
  613.1 55.1 reduce-scatter.21
  671.0 42.4 reduce-scatter.17
  717.5 85.0 reduce-scatter.19
where the time goes:
time: 815 us; the launch traced here: 812 us
  waiting for transfers between devices  508 us (62%)
  matrix products  191 us (23%)
  other arithmetic  68.6 us (8%)
  local copies, waits for them, and re-layouts  27.8 us (3%)
  between operations  14.9 us (2%)
    dot_general x23, matrix products, product(): return jnp.einsum(form, left, right, preferred_element_type=jnp.float32)  107 us
    reduce_scatter x1, waiting for transfers between devices, on_device(): lax.psum_scatter(mixer_full, 'dp', scatter_dimension=1, tiled=True)  84.4 us
    reduce_scatter x1, waiting for transfers between devices, on_device(): lax.psum_scatter(outer_grad, 'dp', scatter_dimension=1, tiled=True)  62.6 us
    reduce_scatter x1, waiting for transfers between devices, on_device(): lax.psum_scatter(output_grad, 'dp', scatter_dimension=1, tiled=True)  57.4 us
    reduce_scatter x1, waiting for transfers between devices, on_device(): lax.psum_scatter(product('wte,de->wtd', grad_query, query_low).astype(jnp...  43.8 us
    reduce_scatter x1, waiting for transfers between devices, on_device(): lax.psum_scatter(product('wtf,df->wtd', grad_pre, inner_low).astype(jnp.b...  43.1 us
    reduce_scatter x1, waiting for transfers between devices, on_device(): lax.psum_scatter(product('wtf,fd->wtd', hidden, outer_low).astype(jnp.bfl...  42.8 us
    reduce_scatter x1, waiting for transfers between devices, on_device(): lax.psum_scatter(product('wte,ed->wtd', field, output_low).astype(jnp.bfl...  42.7 us
  transfers between devices with their start and end apart: 13, of which 13 were waited for; matrix products, arithmetic and copies ran while one was open for 22% of the time, Pallas kernels for 0%

commit v1 on v0

--- a/solution.py
+++ b/solution.py
@@ -102,6 +102,55 @@
     windows, length, local_width = inputs.shape
     head_count, mode_count = modes.shape
     head_size = local_width // head_count
+    hidden_width = inner_weight.shape[1]
+    head_parts = lax.axis_size("head")
+    me = lax.axis_index("head")
+    shifts = list(range(1, head_parts))
+
+    def peer(shift):
+        return (me + shift) % head_parts
+
+    def swap(values, shift):
+        pairs = [(j, (j + shift) % head_parts) for j in range(head_parts)]
+        return lax.ppermute(values, "head", pairs)
+
+    def rows_of(weight, block, size):
+        return lax.dynamic_slice_in_dim(weight, block * size, size, 0)
+
+    def cols_of(weight, block, size):
+        return lax.dynamic_slice_in_dim(weight, block * size, size, 1)
+
+    def gathered_product(mine, weight_low, size):
+        received = {s: swap(mine, s) for s in shifts}
+        total = product("wtd,de->wte", mine, rows_of(weight_low, me, size))
+        for s in shifts:
+            owner = (me - s) % head_parts
+            total = total + product("wtd,de->wte", received[s], rows_of(weight_low, owner, size))
+        return total, received
+
+    def scattered_product(values, weight_low, size):
+        sent = {
+            s: swap(product("wte,ed->wtd", values, cols_of(weight_low, peer(s), size)).astype(jnp.bfloat16), s)
+            for s in shifts
+        }
+        total = product("wte,ed->wtd", values, cols_of(weight_low, me, size))
+        for s in shifts:
+            total = total + sent[s].astype(jnp.float32)
+        return total
+
+    def placed_rows(parts, size, total_rows):
+        out = jnp.zeros((total_rows,) + parts[0][1].shape[1:], jnp.float32)
+        for block, part in parts:
+            out = lax.dynamic_update_slice_in_dim(out, part, block * size, 0)
+        return out
+
+    def placed_cols(parts, size, total_cols):
+        out = jnp.zeros(parts[0][1].shape[:1] + (total_cols,), jnp.float32)
+        for block, part in parts:
+            out = lax.dynamic_update_slice_in_dim(out, part, block * size, 1)
+        return out
+
+    model_width = local_width * head_parts
     pools = pool_tables(length)
     fwd_cos, fwd_sin, inv_cos, inv_sin = [
         one_table.astype(jnp.bfloat16) for one_table in spectral_tables(modes, length)
@@ -111,8 +160,14 @@
     inner_low = inner_weight.astype(jnp.bfloat16)
     outer_low = outer_weight.astype(jnp.bfloat16)
     block = mixer_block(mixer_weight.astype(jnp.bfloat16), head_size)
-    inputs_full = lax.all_gather(inputs.astype(jnp.bfloat16), "head", axis=2, tiled=True)
-    query = product("wtd,de->wte", inputs_full, query_low).astype(jnp.bfloat16)
+
+    grad_comb = out_grad - trend_back(out_grad, gates[1], pools)
+    grad_feed_mine = grad_comb.astype(jnp.bfloat16)
+    grad_feed_recv = {s: swap(grad_feed_mine, s) for s in shifts}
+
+    inputs_mine = inputs.astype(jnp.bfloat16)
+    query, inputs_recv = gathered_product(inputs_mine, query_low, local_width)
+    query = query.astype(jnp.bfloat16)
     query_heads = query.reshape(windows, length, head_count, head_size)
     spectrum = jnp.concatenate(
         [
@@ -126,42 +181,52 @@
         "htm,whme->wthe", inv_sin, mixed[..., head_size:]
     )
     field = field.reshape(windows, length, local_width).astype(jnp.bfloat16)
-    attended = lax.psum_scatter(
-        product("wte,ed->wtd", field, output_low).astype(jnp.bfloat16),
-        "head",
-        scatter_dimension=2,
-        tiled=True,
-    ).astype(jnp.float32)
+    attended = scattered_product(field, output_low, local_width)
     resid_one = inputs + attended
     seasonal = resid_one - trend_local(resid_one, gates[0], pools)
-    seasonal_full = lax.all_gather(seasonal.astype(jnp.bfloat16), "head", axis=2, tiled=True)
-    pre = product("wtd,df->wtf", seasonal_full, inner_low)
+    seasonal_mine = seasonal.astype(jnp.bfloat16)
+    pre, seasonal_recv = gathered_product(seasonal_mine, inner_low, local_width)
     activated, gelu_pull = jax.vjp(exact_gelu, pre)
     hidden = activated.astype(jnp.bfloat16)
-    feed = lax.psum_scatter(
-        product("wtf,fd->wtd", hidden, outer_low).astype(jnp.bfloat16),
-        "head",
-        scatter_dimension=2,
-        tiled=True,
-    ).astype(jnp.float32)
+    feed = scattered_product(hidden, outer_low, local_width)
     combined = seasonal + feed
     output = combined - trend_local(combined, gates[1], pools)
-    grad_comb = out_grad - trend_back(out_grad, gates[1], pools)
-    grad_feed = lax.all_gather(grad_comb.astype(jnp.bfloat16), "head", axis=2, tiled=True)
-    outer_grad = product("wtf,wtd->fd", hidden, grad_feed)
-    grad_hidden = product("wtd,fd->wtf", grad_feed, outer_low)
+
+    outer_grad = placed_cols(
+        [(me, product("wtf,wtd->fd", hidden, grad_feed_mine))]
+        + [((me - s) % head_parts, product("wtf,wtd->fd", hidden, grad_feed_recv[s])) for s in shifts],
+        local_width,
+        model_width,
+    )
+    grad_hidden = product("wtd,fd->wtf", grad_feed_mine, cols_of(outer_low, me, local_width))
+    for s in shifts:
+        grad_hidden = grad_hidden + product(
+            "wtd,fd->wtf", grad_feed_recv[s], cols_of(outer_low, (me - s) % head_parts, local_width)
+        )
     grad_pre = gelu_pull(grad_hidden)[0].astype(jnp.bfloat16)
-    inner_grad = product("wtd,wtf->df", seasonal_full, grad_pre)
-    grad_season = grad_comb + lax.psum_scatter(
-        product("wtf,df->wtd", grad_pre, inner_low).astype(jnp.bfloat16),
-        "head",
-        scatter_dimension=2,
-        tiled=True,
-    ).astype(jnp.float32)
+    inner_grad = placed_rows(
+        [(me, product("wtd,wtf->df", seasonal_mine, grad_pre))]
+        + [((me - s) % head_parts, product("wtd,wtf->df", seasonal_recv[s], grad_pre)) for s in shifts],
+        local_width,
+        model_width,
+    )
+    inner_t = jnp.transpose(inner_low)
+    grad_season = grad_comb + scattered_product(grad_pre, inner_t, local_width)
     grad_resid = grad_season - trend_back(grad_season, gates[0], pools)
-    grad_attend = lax.all_gather(grad_resid.astype(jnp.bfloat16), "head", axis=2, tiled=True)
-    output_grad = product("wte,wtd->ed", field, grad_attend)
-    grad_field = product("wtd,ed->wte", grad_attend, output_low).astype(jnp.bfloat16)
+    grad_attend_mine = grad_resid.astype(jnp.bfloat16)
+    grad_attend_recv = {s: swap(grad_attend_mine, s) for s in shifts}
+    output_grad = placed_cols(
+        [(me, product("wte,wtd->ed", field, grad_attend_mine))]
+        + [((me - s) % head_parts, product("wte,wtd->ed", field, grad_attend_recv[s])) for s in shifts],
+        local_width,
+        model_width,
+    )
+    grad_field = product("wtd,ed->wte", grad_attend_mine, cols_of(output_low, me, local_width))
+    for s in shifts:
+        grad_field = grad_field + product(
+            "wtd,ed->wte", grad_attend_recv[s], cols_of(output_low, (me - s) % head_parts, local_width)
+        )
+    grad_field = grad_field.astype(jnp.bfloat16)
     grad_field = grad_field.reshape(windows, length, head_count, head_size)
     grad_mixed = jnp.concatenate(
         [
@@ -175,30 +240,49 @@
         "hmt,whme->wthe", fwd_sin, grad_spectrum[..., head_size:]
     )
     grad_query = grad_query.reshape(windows, length, local_width).astype(jnp.bfloat16)
-    query_grad = product("wtd,wte->de", inputs_full, grad_query)
-    input_grad = grad_resid + lax.psum_scatter(
-        product("wte,de->wtd", grad_query, query_low).astype(jnp.bfloat16),
-        "head",
-        scatter_dimension=2,
-        tiled=True,
-    ).astype(jnp.float32)
-    query_part, inner_part = (
-        lax.psum_scatter(query_grad, "dp", scatter_dimension=0, tiled=True),
-        lax.psum_scatter(inner_grad, "dp", scatter_dimension=0, tiled=True),
-    )
+    query_grad = placed_rows(
+        [(me, product("wtd,wte->de", inputs_mine, grad_query))]
+        + [((me - s) % head_parts, product("wtd,wte->de", inputs_recv[s], grad_query)) for s in shifts],
+        local_width,
+        model_width,
+    )
+    query_t = jnp.transpose(query_low)
+    input_grad = grad_resid + scattered_product(grad_query, query_t, local_width)
     block_grad = product("whmi,whmo->hmio", spectrum, grad_mixed)
     real_grad = block_grad[:, :, :head_size, :head_size] + block_grad[:, :, head_size:, head_size:]
     imag_grad = block_grad[:, :, :head_size, head_size:] - block_grad[:, :, head_size:, :head_size]
     mixer_full = jnp.concatenate([real_grad, imag_grad], axis=-1).reshape(
         head_count, mode_count * head_size, 2 * head_size
     )
-    mixer_part, output_part, outer_part = (
-        lax.psum_scatter(mixer_full, "dp", scatter_dimension=1, tiled=True),
-        lax.psum_scatter(output_grad, "dp", scatter_dimension=1, tiled=True),
-        lax.psum_scatter(outer_grad, "dp", scatter_dimension=1, tiled=True),
-    )
+
     dp_count = lax.axis_size("dp")
     dp_rank = lax.axis_index("dp")
+
+    def lead(grad, axis_number):
+        shape = grad.shape
+        split = shape[:axis_number] + (dp_count, shape[axis_number] // dp_count) + shape[axis_number + 1 :]
+        owned_shape = shape[:axis_number] + (shape[axis_number] // dp_count,) + shape[axis_number + 1 :]
+        return jnp.moveaxis(grad.reshape(split), axis_number, 0).reshape(dp_count, -1), owned_shape
+
+    laid = [
+        lead(query_grad, 0),
+        lead(mixer_full, 1),
+        lead(output_grad, 1),
+        lead(inner_grad, 0),
+        lead(outer_grad, 1),
+    ]
+    joined = jnp.concatenate([flat for flat, _ in laid], axis=1)
+    lanes = 128
+    reduced = lax.psum_scatter(
+        joined.reshape(-1, lanes), "dp", scatter_dimension=0, tiled=True
+    ).reshape(-1)
+    parts = []
+    offset = 0
+    for flat, owned_shape in laid:
+        size = flat.shape[1]
+        parts.append(reduced[offset : offset + size].reshape(owned_shape))
+        offset += size
+    query_part, mixer_part, output_part, inner_part, outer_part = parts
     token_total = windows * length * dp_count
 
     def owned(weight, share, axis_number):

time: 815 us -> 575 us (0.71)
  waiting for transfers between devices: 508 us -> 177 us
  local copies, waits for them, and re-layouts: 27.8 us -> 84.8 us
  matrix products: 191 us -> 213 us
  starting transfers between devices: 1.29 us -> 10.1 us
    reduce_scatter x9 -> x1, waiting for transfers between devices: 420 us -> 50.9 us  [on_device(): lax.psum_scatter(joined.reshape(-1, lanes), 'dp', scatter_dimension=0, ti...]
    ppermute x0 -> x8, waiting for transfers between devices: none -> 126 us  [swap(): return lax.ppermute(values, 'head', pairs)]
    all_gather x4 -> x0, waiting for transfers between devices: 87.8 us -> none  [the longest x1 40.5 us: on_device(): lax.all_gather(inputs.astype(jnp.bfloat16), 'head', axis=2, tiled=True)]
    dot_general x23 -> x35, matrix products: 107 us -> 131 us  [product(): return jnp.einsum(form, left, right, preferred_element_type=jnp.float32)]
    reshape x0 -> x7, local copies, waits for them, and re-layouts: none -> 21.5 us  [the longest x1 12 us: on_device(): joined.reshape(-1, lanes)]
    unnamed x93 -> x170, local copies, waits for them, and re-layouts: 13.1 us -> 28.9 us
    ppermute x0 -> x8, starting transfers between devices: none -> 10.1 us  [swap(): return lax.ppermute(values, 'head', pairs)]
    another operation x0 -> x3, local copies, waits for them, and re-layouts: none -> 10.1 us  [the longest x1 6.12 us: lead(): grad.reshape(split)]
  transfers between devices with their start and end apart: 13 -> 9, of which waited for: 13 -> 8; matrix products, arithmetic and copies ran while one was open for 22% -> 26% of each run, Pallas kernels for 0% -> 0%
where the time goes in v1:
time: 575 us; the launch traced here: 568 us
  matrix products  213 us (37%)
  waiting for transfers between devices  177 us (31%)
  local copies, waits for them, and re-layouts  84.8 us (15%)
  other arithmetic  67.2 us (12%)
  between operations  15.6 us (3%)
  starting transfers between devices  10.1 us (2%)
    dot_general x35, matrix products, product(): return jnp.einsum(form, left, right, preferred_element_type=jnp.float32)  131 us
    ppermute x8, waiting for transfers between devices, swap(): return lax.ppermute(values, 'head', pairs)  126 us
    reduce_scatter x1, waiting for transfers between devices, on_device(): lax.psum_scatter(joined.reshape(-1, lanes), 'dp', scatter_dimension=0, ti...  50.9 us
    dot_general x10, matrix products, trend_local(): jnp.einsum('ts,wsd->wtd', pools[pool_index], values, precision=highest)  43.2 us
    dot_general x10, matrix products, trend_back(): jnp.einsum('ts,wtd->wsd', pools[pool_index], chosen * grads, precision=hi...  38.9 us
    convert_element_type x1, other arithmetic, on_device(): hidden = activated.astype(jnp.bfloat16)  30.4 us
    unnamed x170, local copies, waits for them, and re-layouts  28.9 us
    reshape x1, local copies, waits for them, and re-layouts, on_device(): joined.reshape(-1, lanes)  12 us
  transfers between devices with their start and end apart: 9, of which 8 were waited for; matrix products, arithmetic and copies ran while one was open for 26% of the time, Pallas kernels for 0%

profile of v1, /device:TPU:0, one launch (start us, length us, event | category | flops | bytes accessed | tf_op | source)
XLA Modules:
  0.0 567.9 jit_solution(4077128653671241183)
XLA Ops:
  7.2 3.3 convert_element_type.229
  10.6 3.0 collective-permute-start
  13.6 3.3 convert_element_type.227
  20.1 4.0 slice_negate_fusion
  24.1 24.2 %collective-permute-done = bf16[32,96,256]{2,1,0:T(8,128)(2,1)} collective-permute-done((bf16[32,96,256]{2,1,0:T(8,128)(2,1)}, bf16[32,96,256]{2,1,0:T(8,128)(2,1)}, u32[]{:S(2)}, u32[]{:S(2)}) %collective-permute-start) | collective-permute-done | bytes 1572896 | tf_op jit(solution)/shard_map/ppermute | solution.py:115
  48.3 3.1 fusion.68
  51.4 3.8 copy.108
  55.2 3.9 fusion.77
  63.4 3.3 fusion.70
  74.1 3.2 fusion.16
  77.4 3.2 fusion.18
  80.6 3.6 fusion.24
  84.3 3.2 fusion.22
  87.5 20.2 %collective-permute-done.1 = bf16[32,96,256]{2,1,0:T(8,128)(2,1)S(1)} collective-permute-done((bf16[32,96,256]{2,1,0:T(8,128)(2,1)S(1)}, bf16[32,96,256]{2,1,0:T(8,128)(2,1)S(1)}, u32[]{:S(2)}, u32[]{:S(2)}) %collective-permute-start.1) | collective-permute-done | bytes 1572896 | tf_op jit(solution)/shard_map/ppermute | solution.py:115
  108.7 3.0 fusion.221
  111.6 4.8 fusion.219
  116.4 4.6 fusion.218
  121.0 4.6 fusion.220
  125.7 7.6 %fusion.215 = (bf16[32,96,256]{2,1,0:T(8,128)(2,1)S(1)}, f32[32,96,256]{2,1,0:T(8,128)}) fusion(f32[32,96,256]{2,1,0:T(8,128)S(1)} %add_add_fusion.3, f32[96,96,1]{1,0,2:T(8,128)S(1)} %copy-done.34, f32[32,96]{1,0:T(8,128)S(1)} %get-tuple-element.86, f32[32,256,96]{1,2,0:T(8,128)S(1)} %fusion.221, f32[32,96]{1,0:T(8,128)S(1)} %get-tuple-element.85, ...), kind=kOutput, calls=%fused_computation.269 | convolution fusion | flops 914620416 | bytes 20545536 | tf_op jit(solution)/shard_map/ts,wsd->wtd/dot_general | solution.py:51
  134.8 5.8 %fusion.216 = (bf16[32,96,256]{2,1,0:T(8,128)(2,1)S(1)}, f32[32,96,256]{2,1,0:T(8,128)}) fusion(f32[32,96,256]{2,1,0:T(8,128)S(1)} %copy-done.1, f32[32,256,96]{1,2,0:T(8,128)S(1)} %fusion.16, f32[32,256,96]{1,2,0:T(8,128)S(1)} %fusion.18, f32[96,96,1]{1,0,2:T(8,128)S(1)} %copy-done.37, f32[32,96]{1,0:T(8,128)S(1)} %get-tuple-element.88, ...), kind=kOutput, calls=%fused_computation.270 | convolution fusion | flops 911474688 | bytes 20496384 | tf_op jit(solution)/shard_map/ts,wtd->wsd/dot_general | solution.py:61
  142.9 6.4 %fusion.97 = f32[32,96,1024]{2,1,0:T(8,128)} fusion(bf16[32,96,256]{2,1,0:T(8,128)(2,1)S(1)} %get-tuple-element.97, bf16[1024,512]{1,0:T(8,128)(2,1)S(1)} %convert_element_type.259, s32[]{:T(128)S(6)} %select_n.84), kind=kOutput, calls=%fused_computation.127 | convolution fusion | flops 1610612736 | bytes 14680068 | tf_op jit(solution)/shard_map/wtd,fd->wtf/dot_general | solution.py:44
  151.2 19.4 %collective-permute-done.2 = bf16[32,96,256]{2,1,0:T(8,128)(2,1)S(1)} collective-permute-done((bf16[32,96,256]{2,1,0:T(8,128)(2,1)S(1)}, bf16[32,96,256]{2,1,0:T(8,128)(2,1)S(1)}, u32[]{:S(2)}, u32[]{:S(2)}) %collective-permute-start.2) | collective-permute-done | bytes 1572896 | tf_op jit(solution)/shard_map/ppermute | solution.py:115
  170.6 7.9 %convert_reduce_fusion.1 = (u32[96,1024]{1,0:T(8,128)S(1)}, u32[96,1024]{1,0:T(8,128)S(1)}, f32[32,96,1024]{2,1,0:T(8,128)}) fusion(f32[32,96,1024]{2,1,0:T(8,128)S(1)} %fusion.106, bf16[32,96,256]{2,1,0:T(8,128)(2,1)S(1)} %collective-permute-done.2, bf16[512,1024]{1,0:T(8,128)(2,1)S(1)} %convert_element_type.257, s32[]{:T(128)S(6)} %select_n.86), kind=kOutput, calls=%fused_computation.6 | convolution fusion | flops 1648164864 | bytes 28049412 | tf_op jit(solution)/shard_map/wtd,de->wte/dot_general | solution.py:44
  178.5 30.4 %multiply_convert_fusion = (bf16[32,96,1024]{2,1,0:T(8,128)(2,1)}, f32[32,96,1024]{2,1,0:T(8,128)}) fusion(f32[32,96,1024]{2,1,0:T(8,128)} %get-tuple-element.96, u32[96,1024]{1,0:T(8,128)S(1)} %get-tuple-element.52, u32[96,1024]{1,0:T(8,128)S(1)} %get-tuple-element.51), kind=kLoop, calls=%fused_computation.8 | loop fusion | flops 213909504 | bytes 32243712 | tf_op jit(solution)/shard_map/convert_element_type | solution.py:190
  208.9 16.8 %add_convert_fusion = bf16[32,96,1024]{2,1,0:T(8,128)(2,1)} fusion(f32[32,96,1024]{2,1,0:T(8,128)} %get-tuple-element.67, f32[32,96,1024]{2,1,0:T(8,128)} %fusion.97, f32[32,96,1024]{2,1,0:T(8,128)} %get-tuple-element.96, bf16[32,96,256]{2,1,0:T(8,128)(2,1)} %collective-permute-done.4, bf16[1024,512]{1,0:T(8,128)(2,1)S(1)} %convert_element_type.259, ...), kind=kOutput, calls=%fused_computation.7 | convolution fusion | flops 1657798656 | bytes 46137348 | tf_op jit(solution)/shard_map/wtd,fd->wtf/dot_general | solution.py:44
  225.8 6.0 %convolution_convert_fusion.3 = bf16[32,96,256]{2,1,0:T(8,128)(2,1)} fusion(bf16[32,96,1024]{2,1,0:T(8,128)(2,1)} %add_convert_fusion, bf16[512,1024]{1,0:T(8,128)(2,1)} %copy-done.22, s32[]{:T(128)S(6)} %select_n.91), kind=kOutput, calls=%fused_computation.75 | convolution fusion | flops 1611399168 | bytes 8388612 | tf_op jit(solution)/shard_map/wte,ed->wtd/dot_general | solution.py:44
  234.9 2.8 fusion.91
  237.7 2.8 fusion.90
  240.5 3.0 reshape_reshape.11
  243.6 19.8 %collective-permute-done.5 = bf16[32,96,256]{2,1,0:T(8,128)(2,1)} collective-permute-done((bf16[32,96,256]{2,1,0:T(8,128)(2,1)}, bf16[32,96,256]{2,1,0:T(8,128)(2,1)}, u32[]{:S(2)}, u32[]{:S(2)}) %collective-permute-start.5) | collective-permute-done | bytes 1572896 | tf_op jit(solution)/shard_map/ppermute | solution.py:115
  263.4 6.1 %add_add_fusion.1 = f32[32,96,256]{2,1,0:T(8,128)S(1)} fusion(f32[32,96,256]{2,1,0:T(8,128)} %get-tuple-element.98, bf16[32,96,256]{2,1,0:T(8,128)(2,1)} %collective-permute-done.5, bf16[32,96,1024]{2,1,0:T(8,128)(2,1)} %add_convert_fusion, bf16[512,1024]{1,0:T(8,128)(2,1)S(1)} %copy-done.23, s32[]{:T(128)S(6)} %select_n.84), kind=kOutput, calls=%fused_computation.46 | convolution fusion | flops 1612972032 | bytes 14680068 | tf_op jit(solution)/shard_map/wte,ed->wtd/dot_general | solution.py:44
  269.6 3.4 fusion.8
  273.0 3.4 fusion.10
  276.4 3.4 fusion.14
  279.8 3.8 fusion.12
  283.6 5.9 %fusion.217 = (bf16[32,96,256]{2,1,0:T(8,128)(2,1)}, f32[32,96,256]{2,1,0:T(8,128)}) fusion(f32[32,96,256]{2,1,0:T(8,128)S(1)} %add_add_fusion.1, f32[96,96,1]{1,0,2:T(8,128)S(1)} %copy-done.34, f32[32,96]{1,0:T(8,128)S(1)} %copy-done.60, f32[32,256,96]{1,2,0:T(8,128)S(1)} %fusion.8, f32[32,256,96]{1,2,0:T(8,128)S(1)} %fusion.10, ...), kind=kOutput, calls=%fused_computation.271 | convolution fusion | flops 911474688 | bytes 20496384 | tf_op jit(solution)/shard_map/ts,wtd->wsd/dot_general | solution.py:61
  292.6 3.3 fusion.88
  297.3 6.3 %copy.146 = f32[16,1024,32]{2,1,0:T(8,128)} copy(f32[16,1024,32]{1,2,0:T(8,128)} %bitcast.270) | data formatting | bytes 4194304 | tf_op jit(solution)/shard_map/transpose | solution.py:265
  303.6 7.0 %reshape.202 = f32[16,32768]{1,0:T(8,128)} reshape(f32[16,1024,32]{2,1,0:T(8,128)} %copy.146) | data formatting | bytes 4194304 | tf_op jit(solution)/shard_map/reshape | solution.py:265
  310.6 2.4 fusion.93
  315.0 5.3 collective-permute-done.6
  320.3 3.2 add_convert_fusion.3
  323.5 4.1 copy.127
  327.6 3.9 fusion.71
  335.7 8.8 %fusion.69 = bf16[32,4,48,128]{3,0,2,1:T(8,128)(2,1)} fusion(bf16[32,4,48,128]{3,2,0,1:T(8,128)(2,1)} %pad_maximum_fusion.2, bf16[4,48,64,64]{3,2,1,0:T(8,128)(2,1)} %get-tuple-element.71, bf16[4,48,64,64]{3,2,1,0:T(8,128)(2,1)} %get-tuple-element.70, bf16[4,48,64,128]{3,2,1,0:T(8,128)(2,1)} %bitcast.257), kind=kOutput, calls=%fused_computation.99 | convolution fusion | flops 220987392 | bytes 9437184 | tf_op jit(solution)/shard_map/whmo,hmio->whmi/dot_general | solution.py:44
  344.5 8.4 %fusion.83 = f32[4,48,128,128]{3,2,1,0:T(8,128)} fusion(bf16[32,4,48,128]{3,2,0,1:T(8,128)(2,1)} %pad_maximum_fusion.2, bf16[32,4,48,128]{3,2,0,1:T(8,128)(2,1)} %copy-done.12), kind=kOutput, calls=%fused_computation.105 | convolution fusion | flops 201326592 | bytes 15728640 | tf_op jit(solution)/shard_map/whmi,whmo->hmio/dot_general | solution.py:44
  360.8 2.7 convolution_bitcast_fusion.6
  368.1 10.0 %slice_add_fusion = (f32[4,48,64,64]{3,2,1,0:T(8,128)S(1)}, f32[4,48,64,64]{3,2,1,0:T(8,128)S(1)}) fusion(f32[4,48,128,128]{3,2,1,0:T(8,128)} %fusion.83), kind=kLoop, calls=%fused_computation.23 | loop fusion | flops 1572864 | bytes 18874368 | tf_op jit(solution)/shard_map/add | solution.py:252
  378.1 4.4 pad_maximum_fusion
  382.5 6.1 %copy.142 = f32[4,16,192,128]{3,2,0,1:T(8,128)} copy(f32[4,16,192,128]{3,2,1,0:T(8,128)} %bitcast.259) | data formatting | bytes 12582912 | tf_op jit(solution)/shard_map/reshape;reshape | solution.py:265
  388.6 2.3 fusion.92
  392.5 9.2 %bitcast_dynamic-update-slice_fusion = f32[16,180224]{1,0:T(8,128)} fusion(f32[16,180224]{1,0:T(8,128)} %constant_dynamic-update-slice_fusion.3, f32[2,8,768,128]{3,2,1,0:T(8,128)} %bitcast.258), kind=kLoop, calls=%fused_computation.21 | loop fusion | bytes 12582912
  405.7 12.0 %reshape.203 = f32[22528,128]{1,0:T(8,128)} reshape(f32[16,180224]{1,0:T(8,128)} %constant_dynamic-update-slice_fusion) | data formatting | bytes 23068672 | tf_op jit(solution)/shard_map/reshape | solution.py:277
  417.8 6.0 %convolution_convert_fusion.4 = bf16[32,96,256]{2,1,0:T(8,128)(2,1)} fusion(bf16[32,96,1024]{2,1,0:T(8,128)(2,1)} %get-tuple-element.66, bf16[1024,512]{1,0:T(8,128)(2,1)} %copy-done.21, s32[]{:T(128)S(6)} %select_n.91), kind=kOutput, calls=%fused_computation.76 | convolution fusion | flops 1611399168 | bytes 8388612 | tf_op jit(solution)/shard_map/wte,ed->wtd/dot_general | solution.py:44
  428.9 24.7 %collective-permute-done.3 = bf16[32,96,256]{2,1,0:T(8,128)(2,1)} collective-permute-done((bf16[32,96,256]{2,1,0:T(8,128)(2,1)}, bf16[32,96,256]{2,1,0:T(8,128)(2,1)}, u32[]{:S(2)}, u32[]{:S(2)}) %collective-permute-start.3) | collective-permute-done | bytes 1572896 | tf_op jit(solution)/shard_map/ppermute | solution.py:115
  453.6 5.3 add_add_fusion.2
  459.0 3.1 fusion.225
  463.3 3.1 fusion.224
  466.4 3.3 fusion.223
  469.8 3.1 fusion.222
  472.9 6.0 %bitcast_subtract_fusion.2 = f32[32,96,256]{2,1,0:T(8,128)} fusion(f32[32,96,256]{2,1,0:T(8,128)S(1)} %add_add_fusion.2, f32[32,256,96]{1,2,0:T(8,128)S(1)} %fusion.225, f32[32,256,96]{1,2,0:T(8,128)S(1)} %fusion.224, f32[32,256,96]{1,2,0:T(8,128)S(1)} %fusion.223, f32[32,256,96]{1,2,0:T(8,128)S(1)} %fusion.222, f32[96,96,1]{1,0,2:T(8,128)S(1)} %copy-done.34, ...), kind=kOutput, calls=%fused_computation.32 | convolution fusion | flops 913833984 | bytes 18972672 | tf_op jit(solution)/shard_map/ts,wsd->wtd/dot_general | solution.py:51
  479.0 12.7 %collective-permute-done.7 = bf16[32,96,256]{2,1,0:T(8,128)(2,1)S(1)} collective-permute-done((bf16[32,96,256]{2,1,0:T(8,128)(2,1)S(1)}, bf16[32,96,256]{2,1,0:T(8,128)(2,1)S(1)}, u32[]{:S(2)}, u32[]{:S(2)}) %collective-permute-start.7) | collective-permute-done | bytes 1572896 | tf_op jit(solution)/shard_map/ppermute | solution.py:115
  491.7 2.5 add_add_fusion
  494.2 50.9 %reduce-scatter.2.cloned.1.call-done = f32[1408,128]{1,0:T(8,128)} async-done(((f32[22528,128]{1,0:T(8,128)}), f32[1408,128]{1,0:T(8,128)}) %reduce-scatter.2.cloned.1.call-update) | async-done | bytes 720912 | tf_op jit(solution)/shard_map/reduce_scatter | solution.py:276
  (231 shorter events, 75.0 us)
Async XLA Ops:
  7.2 6.4 %copy-start.43 = (f32[512,256]{1,0:T(8,128)S(1)}, f32[512,256]{1,0:T(8,128)}, u32[]{:S(2)}) copy-start(f32[512,256]{1,0:T(8,128)} %param.24) | copy-start | bytes 1572868
  7.2 537.8 %reduce-scatter.2.cloned.1.call-start = ((), (), s32[]{:S(2)}) async-start(), calls=%async_computation.1 | async-start | bytes 12255232 | tf_op jit(solution)/shard_map/reduce_scatter | solution.py:276
  10.6 37.7 %collective-permute-start = (bf16[32,96,256]{2,1,0:T(8,128)(2,1)}, bf16[32,96,256]{2,1,0:T(8,128)(2,1)}, u32[]{:S(2)}, u32[]{:S(2)}) collective-permute-start(bf16[32,96,256]{2,1,0:T(8,128)(2,1)} %convert_element_type.229), channel_id=1, source_target_pairs={{0,1},{1,0},{2,3},{3,2},{4,5},{5,4},{6,7},{7,6},{8,9},{9,8},{10,11... | collective-permute-start | bytes 4718600 | tf_op jit(solution)/shard_map/ppermute | solution.py:115
  13.6 34.7 %copy-start.28 = (bf16[512,256]{1,0:T(8,128)(2,1)}, bf16[512,256]{1,0:T(8,128)(2,1)S(1)}, u32[]{:S(2)}) copy-start(bf16[512,256]{1,0:T(8,128)(2,1)S(1)} %convert_element_type.228) | copy-start | bytes 786436
  13.6 4.1 copy-start.47
  16.9 45.4 %copy-start.2 = (bf16[4,3072,128]{2,1,0:T(8,128)(2,1)}, bf16[4,3072,128]{2,1,0:T(8,128)(2,1)S(1)}, u32[]{:S(2)}) copy-start(bf16[4,3072,128]{2,1,0:T(8,128)(2,1)S(1)} %convert_element_type.227) | copy-start | bytes 9437188
  17.8 49.7 %copy-start.72 = (f32[4,48]{1,0:T(4,128)}, f32[4,48]{1,0:T(4,128)S(1)}, u32[]{:S(2)}) copy-start(f32[4,48]{1,0:T(4,128)S(1)} %get-tuple-element.93) | copy-start | bytes 2308
  17.8 51.1 %copy-start.74 = (f32[4,48]{1,0:T(4,128)}, f32[4,48]{1,0:T(4,128)S(1)}, u32[]{:S(2)}) copy-start(f32[4,48]{1,0:T(4,128)S(1)} %get-tuple-element.92) | copy-start | bytes 2308
  55.2 4.0 copy-start.8
  62.3 4.4 copy-start.12
  70.4 3.6 copy-start.71
  70.4 3.7 copy-start.1
  70.4 3.7 copy-start.34
  72.1 35.6 %collective-permute-start.1 = (bf16[32,96,256]{2,1,0:T(8,128)(2,1)S(1)}, bf16[32,96,256]{2,1,0:T(8,128)(2,1)S(1)}, u32[]{:S(2)}, u32[]{:S(2)}) collective-permute-start(bf16[32,96,256]{2,1,0:T(8,128)(2,1)S(1)} %convolution_convert_fusion.5), channel_id=1, source_target_pairs={{0,1},{1,0},{2,3},{3,2},{4,5},{5,4},{6,7},{7,6},{8,9},{9,8},{10,11... | collective-permute-start | bytes 4718600 | tf_op jit(solution)/shard_map/ppermute | solution.py:115
  74.0 6.6 %copy-start.49 = (f32[32,96]{1,0:T(8,128)}, f32[32,96]{1,0:T(8,128)S(1)}, u32[]{:S(2)}) copy-start(f32[32,96]{1,0:T(8,128)S(1)} %get-tuple-element.82) | copy-start | bytes 36868
  74.0 10.3 %copy-start.51 = (f32[32,96]{1,0:T(8,128)}, f32[32,96]{1,0:T(8,128)S(1)}, u32[]{:S(2)}) copy-start(f32[32,96]{1,0:T(8,128)S(1)} %get-tuple-element.87) | copy-start | bytes 36868
  74.0 51.6 %copy-start.59 = (f32[32,96]{1,0:T(8,128)}, f32[32,96]{1,0:T(8,128)S(1)}, u32[]{:S(2)}) copy-start(f32[32,96]{1,0:T(8,128)S(1)} %get-tuple-element.86) | copy-start | bytes 36868
  74.0 51.6 %copy-start.61 = (f32[32,96]{1,0:T(8,128)}, f32[32,96]{1,0:T(8,128)S(1)}, u32[]{:S(2)}) copy-start(f32[32,96]{1,0:T(8,128)S(1)} %get-tuple-element.83) | copy-start | bytes 36868
  74.0 51.6 %copy-start.63 = (f32[32,96]{1,0:T(8,128)}, f32[32,96]{1,0:T(8,128)S(1)}, u32[]{:S(2)}) copy-start(f32[32,96]{1,0:T(8,128)S(1)} %get-tuple-element.91) | copy-start | bytes 36868
  74.0 51.6 %copy-start.65 = (f32[32,96]{1,0:T(8,128)}, f32[32,96]{1,0:T(8,128)S(1)}, u32[]{:S(2)}) copy-start(f32[32,96]{1,0:T(8,128)S(1)} %get-tuple-element.84) | copy-start | bytes 36868
  74.1 51.6 %copy-start.67 = (f32[32,96]{1,0:T(8,128)}, f32[32,96]{1,0:T(8,128)S(1)}, u32[]{:S(2)}) copy-start(f32[32,96]{1,0:T(8,128)S(1)} %get-tuple-element.85) | copy-start | bytes 36868
  74.1 60.7 %copy-start.53 = (f32[32,96]{1,0:T(8,128)}, f32[32,96]{1,0:T(8,128)S(1)}, u32[]{:S(2)}) copy-start(f32[32,96]{1,0:T(8,128)S(1)} %get-tuple-element.88) | copy-start | bytes 36868
  80.6 3.7 copy-start.36
  84.3 23.5 %copy-start.10 = (f32[32,96,256]{2,1,0:T(8,128)S(1)}, f32[32,96,256]{2,1,0:T(8,128)}, u32[]{:S(2)}) copy-start(f32[32,96,256]{2,1,0:T(8,128)} %param.20) | copy-start | bytes 9437188
  116.4 4.6 copy-start.37
  133.3 16.1 %copy-start.3 = (bf16[32,96,256]{2,1,0:T(8,128)(2,1)}, bf16[32,96,256]{2,1,0:T(8,128)(2,1)S(1)}, u32[]{:S(2)}) copy-start(bf16[32,96,256]{2,1,0:T(8,128)(2,1)S(1)} %get-tuple-element.94) | copy-start | bytes 4718596
  133.3 37.3 %collective-permute-start.2 = (bf16[32,96,256]{2,1,0:T(8,128)(2,1)S(1)}, bf16[32,96,256]{2,1,0:T(8,128)(2,1)S(1)}, u32[]{:S(2)}, u32[]{:S(2)}) collective-permute-start(bf16[32,96,256]{2,1,0:T(8,128)(2,1)S(1)} %get-tuple-element.94), channel_id=1, source_target_pairs={{0,1},{1,0},{2,3},{3,2},{4,5},{5,4},{6,7},{7,6},{8,9},{9,8},{10,11... | collective-permute-start | bytes 4718600 | tf_op jit(solution)/shard_map/ppermute | solution.py:115
  134.8 6.4 %copy-start.27 = (f32[512,1024]{1,0:T(8,128)S(1)}, f32[512,1024]{1,0:T(8,128)}, u32[]{:S(2)}) copy-start(f32[512,1024]{1,0:T(8,128)} %param.27) | copy-start | bytes 6291460
  140.6 68.3 %collective-permute-start.4 = (bf16[32,96,256]{2,1,0:T(8,128)(2,1)S(1)}, bf16[32,96,256]{2,1,0:T(8,128)(2,1)}, u32[]{:S(2)}, u32[]{:S(2)}) collective-permute-start(bf16[32,96,256]{2,1,0:T(8,128)(2,1)S(1)} %get-tuple-element.97), channel_id=1, source_target_pairs={{0,1},{1,0},{2,3},{3,2},{4,5},{5,4},{6,7},{7,6},{8,9},{9,8},{10,11... | collective-permute-start | bytes 4718600 | tf_op jit(solution)/shard_map/ppermute | solution.py:115
  142.8 27.8 %copy-start.22 = (bf16[512,1024]{1,0:T(8,128)(2,1)}, bf16[512,1024]{1,0:T(8,128)(2,1)S(1)}, u32[]{:S(2)}) copy-start(bf16[512,1024]{1,0:T(8,128)(2,1)S(1)} %convert_element_type.257) | copy-start | bytes 3145732
  142.9 66.0 %copy-start.21 = (bf16[1024,512]{1,0:T(8,128)(2,1)}, bf16[1024,512]{1,0:T(8,128)(2,1)S(1)}, u32[]{:S(2)}) copy-start(bf16[1024,512]{1,0:T(8,128)(2,1)S(1)} %convert_element_type.259) | copy-start | bytes 3145732
  170.6 7.9 %copy-start.19 = (bf16[32,96,256]{2,1,0:T(8,128)(2,1)}, bf16[32,96,256]{2,1,0:T(8,128)(2,1)S(1)}, u32[]{:S(2)}) copy-start(bf16[32,96,256]{2,1,0:T(8,128)(2,1)S(1)} %collective-permute-done.2) | copy-start | bytes 4718596
  225.8 9.1 %copy-start = (bf16[32,96,1024]{2,1,0:T(8,128)(2,1)S(1)}, bf16[32,96,1024]{2,1,0:T(8,128)(2,1)}, u32[]{:S(2)}) copy-start(bf16[32,96,1024]{2,1,0:T(8,128)(2,1)} %add_convert_fusion) | copy-start | bytes 18874372
  231.8 31.6 %collective-permute-start.5 = (bf16[32,96,256]{2,1,0:T(8,128)(2,1)}, bf16[32,96,256]{2,1,0:T(8,128)(2,1)}, u32[]{:S(2)}, u32[]{:S(2)}) collective-permute-start(bf16[32,96,256]{2,1,0:T(8,128)(2,1)} %convolution_convert_fusion.3), channel_id=1, source_target_pairs={{0,1},{1,0},{2,3},{3,2},{4,5},{5,4},{6,7},{7,6},{8,9},{9,8},{10,11... | collective-permute-start | bytes 4718600 | tf_op jit(solution)/shard_map/ppermute | solution.py:115
  240.5 22.9 %copy-start.23 = (bf16[512,1024]{1,0:T(8,128)(2,1)S(1)}, bf16[512,1024]{1,0:T(8,128)(2,1)}, u32[]{:S(2)}) copy-start(bf16[512,1024]{1,0:T(8,128)(2,1)} %copy-done.22) | copy-start | bytes 3145732
  263.4 6.2 %copy-start.41 = (f32[96,96,1]{1,0,2:T(8,128)S(1)}, f32[96,96,1]{1,0,2:T(8,128)}, u32[]{:S(2)}) copy-start(f32[96,96,1]{1,0,2:T(8,128)} %constant.189) | copy-start | bytes 110596
  263.4 6.2 %copy-start.68 = (f32[32,96]{1,0:T(8,128)S(1)}, f32[32,96]{1,0:T(8,128)}, u32[]{:S(2)}) copy-start(f32[32,96]{1,0:T(8,128)} %copy-done.67) | copy-start | bytes 36868
  269.5 3.4 copy-start.38
  269.6 3.4 copy-start.66
  273.0 3.4 copy-start.64
  279.8 3.8 copy-start.60
  279.8 10.9 %slice-start = ((s8[6291456]{0:T(1024)(128)(4,1)}), s8[4194304]{0:T(1024)(128)(4,1)S(1)}, s32[]{:S(2)}) async-start(s8[6291456]{0:T(1024)(128)(4,1)} %bitcast.260), calls=%async_computation.2 | async-start | bytes 8388608
  283.6 7.1 %slice-start.1 = ((s8[6291456]{0:T(1024)(128)(4,1)}), s8[2097152]{0:T(1024)(128)(4,1)S(1)}, s32[]{:S(2)}) async-start(s8[6291456]{0:T(1024)(128)(4,1)} %bitcast.260), calls=%async_computation.3 | async-start | bytes 4194304
  283.6 7.1 %copy-start.18 = (bf16[32,96,256]{2,1,0:T(8,128)(2,1)S(1)}, bf16[32,96,256]{2,1,0:T(8,128)(2,1)}, u32[]{:S(2)}) copy-start(bf16[32,96,256]{2,1,0:T(8,128)(2,1)} %copy-done.17) | copy-start | bytes 4718596
  289.5 30.7 %collective-permute-start.6 = (bf16[32,96,256]{2,1,0:T(8,128)(2,1)}, bf16[32,96,256]{2,1,0:T(8,128)(2,1)}, u32[]{:S(2)}, u32[]{:S(2)}) collective-permute-start(bf16[32,96,256]{2,1,0:T(8,128)(2,1)} %get-tuple-element.99), channel_id=1, source_target_pairs={{0,1},{1,0},{2,3},{3,2},{4,5},{5,4},{6,7},{7,6},{8,9},{9,8},{10,11... | collective-permute-start | bytes 4718600 | tf_op jit(solution)/shard_map/ppermute | solution.py:115
  323.5 4.1 copy-start.48
  323.5 4.1 copy-start.75
  323.5 8.0 %copy-start.73 = (f32[4,48]{1,0:T(4,128)S(1)}, f32[4,48]{1,0:T(4,128)}, u32[]{:S(2)}) copy-start(f32[4,48]{1,0:T(4,128)} %copy-done.72) | copy-start | bytes 2308
  327.6 4.0 copy-start.7
  344.5 8.4 %copy-start.16 = (bf16[32,4,48,128]{3,0,2,1:T(8,128)(2,1)S(1)}, bf16[32,4,48,128]{3,0,2,1:T(8,128)(2,1)}, u32[]{:S(2)}) copy-start(bf16[32,4,48,128]{3,0,2,1:T(8,128)(2,1)} %fusion.69) | copy-start | bytes 4718596
  392.5 10.1 %copy-start.15 = (f32[16,32768]{1,0:T(8,128)S(1)}, f32[16,32768]{1,0:T(8,128)}, u32[]{:S(2)}) copy-start(f32[16,32768]{1,0:T(8,128)} %reshape_reshape.11) | copy-start | bytes 6291460
  417.7 6.4 %copy-start.69 = (f32[256,32]{0,1:T(8,128)S(1)}, f32[256,32]{0,1:T(8,128)}, u32[]{:S(2)}) copy-start(f32[256,32]{0,1:T(8,128)} %param.34) | copy-start | bytes 98308
  417.7 6.5 %copy-start.70 = (f32[256,32]{0,1:T(8,128)S(1)}, f32[256,32]{0,1:T(8,128)}, u32[]{:S(2)}) copy-start(f32[256,32]{0,1:T(8,128)} %param.33) | copy-start | bytes 98308
  417.8 35.8 %copy-start.11 = (f32[32,96,256]{2,1,0:T(8,128)S(1)}, f32[32,96,256]{2,1,0:T(8,128)}, u32[]{:S(2)}) copy-start(f32[32,96,256]{2,1,0:T(8,128)} %get-tuple-element.95) | copy-start | bytes 9437188
  423.7 29.9 %collective-permute-start.3 = (bf16[32,96,256]{2,1,0:T(8,128)(2,1)}, bf16[32,96,256]{2,1,0:T(8,128)(2,1)}, u32[]{:S(2)}, u32[]{:S(2)}) collective-permute-start(bf16[32,96,256]{2,1,0:T(8,128)(2,1)} %convolution_convert_fusion.4), channel_id=1, source_target_pairs={{0,1},{1,0},{2,3},{3,2},{4,5},{5,4},{6,7},{7,6},{8,9},{9,8},{10,11... | collective-permute-start | bytes 4718600 | tf_op jit(solution)/shard_map/ppermute | solution.py:115
  453.6 5.3 copy-start.42
  462.9 28.8 %collective-permute-start.7 = (bf16[32,96,256]{2,1,0:T(8,128)(2,1)S(1)}, bf16[32,96,256]{2,1,0:T(8,128)(2,1)S(1)}, u32[]{:S(2)}, u32[]{:S(2)}) collective-permute-start(bf16[32,96,256]{2,1,0:T(8,128)(2,1)S(1)} %convolution_convert_fusion.1), channel_id=1, source_target_pairs={{0,1},{1,0},{2,3},{3,2},{4,5},{5,4},{6,7},{7,6},{8,9},{9,8},{10,11... | collective-permute-start | bytes 4718600 | tf_op jit(solution)/shard_map/ppermute | solution.py:115
  472.9 18.7 %copy-start.9 = (f32[32,96,256]{2,1,0:T(8,128)S(1)}, f32[32,96,256]{2,1,0:T(8,128)}, u32[]{:S(2)}) copy-start(f32[32,96,256]{2,1,0:T(8,128)} %get-tuple-element.100) | copy-start | bytes 9437188
  491.7 54.9 %copy-start.44 = (f32[256,32]{1,0:T(8,128)S(1)}, f32[256,32]{1,0:T(8,128)}, u32[]{:S(2)}) copy-start(f32[256,32]{1,0:T(8,128)} %copy.147) | copy-start | bytes 98308
  494.2 57.3 %copy-start.31 = (f32[1024,32]{1,0:T(8,128)S(1)}, f32[1024,32]{1,0:T(8,128)}, u32[]{:S(2)}) copy-start(f32[1024,32]{1,0:T(8,128)} %copy.150) | copy-start | bytes 393220
  494.2 57.3 %copy-start.32 = (f32[1024,32]{1,0:T(8,128)S(1)}, f32[1024,32]{1,0:T(8,128)}, u32[]{:S(2)}) copy-start(f32[1024,32]{1,0:T(8,128)} %copy.149) | copy-start | bytes 393220
  551.5 7.2 %slice-start.2 = ((f32[1408,128]{1,0:T(8,128)}), f32[768,128]{1,0:T(8,128)S(1)}, s32[]{:S(2)}) async-start(f32[1408,128]{1,0:T(8,128)} %reduce-scatter.2.cloned.1.call-done), calls=%async_computation.4 | async-start | bytes 786432 | tf_op jit(solution)/shard_map/slice | solution.py:283
  552.9 5.8 %copy-start.45 = (f32[4,192,128]{2,1,0:T(8,128)S(1)}, f32[4,192,128]{2,1,0:T(8,128)}, u32[]{:S(2)}) copy-start(f32[4,192,128]{2,1,0:T(8,128)} %param.32) | copy-start | bytes 1179652
  552.9 5.8 %copy-start.46 = (f32[4,192,128]{2,1,0:T(8,128)S(1)}, f32[4,192,128]{2,1,0:T(8,128)}, u32[]{:S(2)}) copy-start(f32[4,192,128]{2,1,0:T(8,128)} %param.31) | copy-start | bytes 1179652
  (24 other events, 64.7 us)
Sparse Core Ops, SparseCore 0:
  417.9 127.1 reduce-scatter.1

commit v2 on v1

--- a/solution.py
+++ b/solution.py
@@ -44,24 +44,19 @@
     return jnp.einsum(form, left, right, preferred_element_type=jnp.float32)
 
 
-def trend_local(values, picks, pools):
-    total = jnp.zeros_like(values)
+def pool_rows(picks, pools):
+    rows = jnp.zeros(picks.shape + (pools.shape[-1],), jnp.float32)
     for pool_index in range(len(pool_sizes)):
-        chosen = (picks == pool_index).astype(jnp.float32)[..., None]
-        total = total + chosen * jnp.einsum(
-            "ts,wsd->wtd", pools[pool_index], values, precision=highest
-        )
-    return total
-
-
-def trend_back(grads, picks, pools):
-    total = jnp.zeros_like(grads)
-    for pool_index in range(len(pool_sizes)):
-        chosen = (picks == pool_index).astype(jnp.float32)[..., None]
-        total = total + jnp.einsum(
-            "ts,wtd->wsd", pools[pool_index], chosen * grads, precision=highest
-        )
-    return total
+        rows = jnp.where((picks == pool_index)[..., None], pools[pool_index][None], rows)
+    return rows
+
+
+def trend_local(values, rows):
+    return jnp.einsum("wts,wsd->wtd", rows, values, precision=highest)
+
+
+def trend_back(grads, rows):
+    return jnp.einsum("wts,wtd->wsd", rows, grads, precision=highest)
 
 
 def mixer_block(mixer_low, head_size):
@@ -159,101 +154,124 @@
     output_low = output_weight.astype(jnp.bfloat16)
     inner_low = inner_weight.astype(jnp.bfloat16)
     outer_low = outer_weight.astype(jnp.bfloat16)
+    inner_t = jnp.transpose(inner_low)
+    query_t = jnp.transpose(query_low)
     block = mixer_block(mixer_weight.astype(jnp.bfloat16), head_size)
 
-    grad_comb = out_grad - trend_back(out_grad, gates[1], pools)
-    grad_feed_mine = grad_comb.astype(jnp.bfloat16)
-    grad_feed_recv = {s: swap(grad_feed_mine, s) for s in shifts}
-
-    inputs_mine = inputs.astype(jnp.bfloat16)
-    query, inputs_recv = gathered_product(inputs_mine, query_low, local_width)
-    query = query.astype(jnp.bfloat16)
-    query_heads = query.reshape(windows, length, head_count, head_size)
-    spectrum = jnp.concatenate(
-        [
-            product("hmt,wthe->whme", fwd_cos, query_heads),
-            product("hmt,wthe->whme", fwd_sin, query_heads),
-        ],
-        axis=-1,
-    ).astype(jnp.bfloat16)
-    mixed = product("whmi,hmio->whmo", spectrum, block).astype(jnp.bfloat16)
-    field = product("htm,whme->wthe", inv_cos, mixed[..., :head_size]) + product(
-        "htm,whme->wthe", inv_sin, mixed[..., head_size:]
-    )
-    field = field.reshape(windows, length, local_width).astype(jnp.bfloat16)
-    attended = scattered_product(field, output_low, local_width)
-    resid_one = inputs + attended
-    seasonal = resid_one - trend_local(resid_one, gates[0], pools)
-    seasonal_mine = seasonal.astype(jnp.bfloat16)
-    pre, seasonal_recv = gathered_product(seasonal_mine, inner_low, local_width)
-    activated, gelu_pull = jax.vjp(exact_gelu, pre)
-    hidden = activated.astype(jnp.bfloat16)
-    feed = scattered_product(hidden, outer_low, local_width)
-    combined = seasonal + feed
-    output = combined - trend_local(combined, gates[1], pools)
-
-    outer_grad = placed_cols(
-        [(me, product("wtf,wtd->fd", hidden, grad_feed_mine))]
-        + [((me - s) % head_parts, product("wtf,wtd->fd", hidden, grad_feed_recv[s])) for s in shifts],
-        local_width,
-        model_width,
-    )
-    grad_hidden = product("wtd,fd->wtf", grad_feed_mine, cols_of(outer_low, me, local_width))
-    for s in shifts:
-        grad_hidden = grad_hidden + product(
-            "wtd,fd->wtf", grad_feed_recv[s], cols_of(outer_low, (me - s) % head_parts, local_width)
-        )
-    grad_pre = gelu_pull(grad_hidden)[0].astype(jnp.bfloat16)
-    inner_grad = placed_rows(
-        [(me, product("wtd,wtf->df", seasonal_mine, grad_pre))]
-        + [((me - s) % head_parts, product("wtd,wtf->df", seasonal_recv[s], grad_pre)) for s in shifts],
-        local_width,
-        model_width,
-    )
-    inner_t = jnp.transpose(inner_low)
-    grad_season = grad_comb + scattered_product(grad_pre, inner_t, local_width)
-    grad_resid = grad_season - trend_back(grad_season, gates[0], pools)
-    grad_attend_mine = grad_resid.astype(jnp.bfloat16)
-    grad_attend_recv = {s: swap(grad_attend_mine, s) for s in shifts}
-    output_grad = placed_cols(
-        [(me, product("wte,wtd->ed", field, grad_attend_mine))]
-        + [((me - s) % head_parts, product("wte,wtd->ed", field, grad_attend_recv[s])) for s in shifts],
-        local_width,
-        model_width,
-    )
-    grad_field = product("wtd,ed->wte", grad_attend_mine, cols_of(output_low, me, local_width))
-    for s in shifts:
-        grad_field = grad_field + product(
-            "wtd,ed->wte", grad_attend_recv[s], cols_of(output_low, (me - s) % head_parts, local_width)
-        )
-    grad_field = grad_field.astype(jnp.bfloat16)
-    grad_field = grad_field.reshape(windows, length, head_count, head_size)
-    grad_mixed = jnp.concatenate(
-        [
-            product("htm,wthe->whme", inv_cos, grad_field),
-            product("htm,wthe->whme", inv_sin, grad_field),
-        ],
-        axis=-1,
-    ).astype(jnp.bfloat16)
-    grad_spectrum = product("whmo,hmio->whmi", grad_mixed, block).astype(jnp.bfloat16)
-    grad_query = product("hmt,whme->wthe", fwd_cos, grad_spectrum[..., :head_size]) + product(
-        "hmt,whme->wthe", fwd_sin, grad_spectrum[..., head_size:]
-    )
-    grad_query = grad_query.reshape(windows, length, local_width).astype(jnp.bfloat16)
-    query_grad = placed_rows(
-        [(me, product("wtd,wte->de", inputs_mine, grad_query))]
-        + [((me - s) % head_parts, product("wtd,wte->de", inputs_recv[s], grad_query)) for s in shifts],
-        local_width,
-        model_width,
-    )
-    query_t = jnp.transpose(query_low)
-    input_grad = grad_resid + scattered_product(grad_query, query_t, local_width)
-    block_grad = product("whmi,whmo->hmio", spectrum, grad_mixed)
-    real_grad = block_grad[:, :, :head_size, :head_size] + block_grad[:, :, head_size:, head_size:]
-    imag_grad = block_grad[:, :, :head_size, head_size:] - block_grad[:, :, head_size:, :head_size]
-    mixer_full = jnp.concatenate([real_grad, imag_grad], axis=-1).reshape(
-        head_count, mode_count * head_size, 2 * head_size
-    )
+    def chunk_pass(inputs, out_grad, first_rows, second_rows):
+        windows = inputs.shape[0]
+        grad_comb = out_grad - trend_back(out_grad, second_rows)
+        grad_feed_mine = grad_comb.astype(jnp.bfloat16)
+        grad_feed_recv = {s: swap(grad_feed_mine, s) for s in shifts}
+
+        inputs_mine = inputs.astype(jnp.bfloat16)
+        query, inputs_recv = gathered_product(inputs_mine, query_low, local_width)
+        query = query.astype(jnp.bfloat16)
+        query_heads = query.reshape(windows, length, head_count, head_size)
+        spectrum = jnp.concatenate(
+            [
+                product("hmt,wthe->whme", fwd_cos, query_heads),
+                product("hmt,wthe->whme", fwd_sin, query_heads),
+            ],
+            axis=-1,
+        ).astype(jnp.bfloat16)
+        mixed = product("whmi,hmio->whmo", spectrum, block).astype(jnp.bfloat16)
+        field = product("htm,whme->wthe", inv_cos, mixed[..., :head_size]) + product(
+            "htm,whme->wthe", inv_sin, mixed[..., head_size:]
+        )
+        field = field.reshape(windows, length, local_width).astype(jnp.bfloat16)
+        attended = scattered_product(field, output_low, local_width)
+        resid_one = inputs + attended
+        seasonal = resid_one - trend_local(resid_one, first_rows)
+        seasonal_mine = seasonal.astype(jnp.bfloat16)
+        pre, seasonal_recv = gathered_product(seasonal_mine, inner_low, local_width)
+        activated, gelu_pull = jax.vjp(exact_gelu, pre)
+        hidden = activated.astype(jnp.bfloat16)
+        feed = scattered_product(hidden, outer_low, local_width)
+        combined = seasonal + feed
+        output = combined - trend_local(combined, second_rows)
+
+        outer_grad = placed_cols(
+            [(me, product("wtf,wtd->fd", hidden, grad_feed_mine))]
+            + [((me - s) % head_parts, product("wtf,wtd->fd", hidden, grad_feed_recv[s])) for s in shifts],
+            local_width,
+            model_width,
+        )
+        grad_hidden = product("wtd,fd->wtf", grad_feed_mine, cols_of(outer_low, me, local_width))
+        for s in shifts:
+            grad_hidden = grad_hidden + product(
+                "wtd,fd->wtf", grad_feed_recv[s], cols_of(outer_low, (me - s) % head_parts, local_width)
+            )
+        grad_pre = gelu_pull(grad_hidden)[0].astype(jnp.bfloat16)
+        inner_grad = placed_rows(
+            [(me, product("wtd,wtf->df", seasonal_mine, grad_pre))]
+            + [((me - s) % head_parts, product("wtd,wtf->df", seasonal_recv[s], grad_pre)) for s in shifts],
+            local_width,
+            model_width,
+        )
+        grad_season = grad_comb + scattered_product(grad_pre, inner_t, local_width)
+        grad_resid = grad_season - trend_back(grad_season, first_rows)
+        grad_attend_mine = grad_resid.astype(jnp.bfloat16)
+        grad_attend_recv = {s: swap(grad_attend_mine, s) for s in shifts}
+        output_grad = placed_cols(
+            [(me, product("wte,wtd->ed", field, grad_attend_mine))]
+            + [((me - s) % head_parts, product("wte,wtd->ed", field, grad_attend_recv[s])) for s in shifts],
+            local_width,
+            model_width,
+        )
+        grad_field = product("wtd,ed->wte", grad_attend_mine, cols_of(output_low, me, local_width))
+        for s in shifts:
+            grad_field = grad_field + product(
+                "wtd,ed->wte", grad_attend_recv[s], cols_of(output_low, (me - s) % head_parts, local_width)
+            )
+        grad_field = grad_field.astype(jnp.bfloat16)
+        grad_field = grad_field.reshape(windows, length, head_count, head_size)
+        grad_mixed = jnp.concatenate(
+            [
+                product("htm,wthe->whme", inv_cos, grad_field),
+                product("htm,wthe->whme", inv_sin, grad_field),
+            ],
+            axis=-1,
+        ).astype(jnp.bfloat16)
+        grad_spectrum = product("whmo,hmio->whmi", grad_mixed, block).astype(jnp.bfloat16)
+        grad_query = product("hmt,whme->wthe", fwd_cos, grad_spectrum[..., :head_size]) + product(
+            "hmt,whme->wthe", fwd_sin, grad_spectrum[..., head_size:]
+        )
+        grad_query = grad_query.reshape(windows, length, local_width).astype(jnp.bfloat16)
+        query_grad = placed_rows(
+            [(me, product("wtd,wte->de", inputs_mine, grad_query))]
+            + [((me - s) % head_parts, product("wtd,wte->de", inputs_recv[s], grad_query)) for s in shifts],
+            local_width,
+            model_width,
+        )
+        input_grad = grad_resid + scattered_product(grad_query, query_t, local_width)
+        block_grad = product("whmi,whmo->hmio", spectrum, grad_mixed)
+        real_grad = block_grad[:, :, :head_size, :head_size] + block_grad[:, :, head_size:, head_size:]
+        imag_grad = block_grad[:, :, :head_size, head_size:] - block_grad[:, :, head_size:, :head_size]
+        mixer_full = jnp.concatenate([real_grad, imag_grad], axis=-1).reshape(
+            head_count, mode_count * head_size, 2 * head_size
+        )
+        return output, input_grad, (query_grad, mixer_full, output_grad, inner_grad, outer_grad)
+
+    chunks = 2 if windows % 2 == 0 else 1
+    span = windows // chunks
+    first_all = pool_rows(gates[0], pools)
+    second_all = pool_rows(gates[1], pools)
+    results = [
+        chunk_pass(
+            inputs[c * span : (c + 1) * span],
+            out_grad[c * span : (c + 1) * span],
+            first_all[c * span : (c + 1) * span],
+            second_all[c * span : (c + 1) * span],
+        )
+        for c in range(chunks)
+    ]
+    output = jnp.concatenate([r[0] for r in results], axis=0)
+    input_grad = jnp.concatenate([r[1] for r in results], axis=0)
+    query_grad, mixer_full, output_grad, inner_grad, outer_grad = [
+        sum(r[2][i] for r in results[1:]) + results[0][2][i] if chunks > 1 else results[0][2][i]
+        for i in range(5)
+    ]
 
     dp_count = lax.axis_size("dp")
     dp_rank = lax.axis_index("dp")

time: 575 us -> 563 us (0.979)
  waiting for transfers between devices: 177 us -> 142 us
  other arithmetic: 67.2 us -> 97.6 us
  matrix products: 213 us -> 198 us
  starting transfers between devices: 10.1 us -> 19.7 us
    dot_general x20 -> x8, matrix products: 82.1 us -> 33.3 us  [the longest x4 21.3 us: trend_back(): return jnp.einsum('wts,wtd->wsd', rows, grads, precision=highest)]
    ppermute x8 -> x16, waiting for transfers between devices: 126 us -> 87.9 us  [swap(): return lax.ppermute(values, 'head', pairs)]
    add x1 -> x6, other arithmetic: 10 us -> 46 us  [the longest x1 27.8 us: chunk_pass(): block_grad[:, :, :head_size, :head_size]]
    dot_general x35 -> x70, matrix products: 131 us -> 165 us  [product(): return jnp.einsum(form, left, right, preferred_element_type=jnp.float32)]
    ppermute x8 -> x16, starting transfers between devices: 10.1 us -> 19.6 us  [swap(): return lax.ppermute(values, 'head', pairs)]
    unnamed x170 -> x210, local copies, waits for them, and re-layouts: 28.9 us -> 21.7 us
    convert_element_type x3 -> x2, other arithmetic: 33.7 us -> 29.8 us  [chunk_pass(): hidden = activated.astype(jnp.bfloat16)]
  transfers between devices with their start and end apart: 9 -> 17, of which waited for: 8 -> 10; matrix products, arithmetic and copies ran while one was open for 26% -> 41% of each run, Pallas kernels for 0% -> 0%
where the time goes in v2:
time: 563 us; the launch traced here: 553 us
  matrix products  198 us (35%)
  waiting for transfers between devices  142 us (25%)
  other arithmetic  97.6 us (17%)
  local copies, waits for them, and re-layouts  80.1 us (14%)
  starting transfers between devices  19.7 us (3%)
  between operations  16.2 us (3%)
    dot_general x70, matrix products, product(): return jnp.einsum(form, left, right, preferred_element_type=jnp.float32)  165 us
    ppermute x16, waiting for transfers between devices, swap(): return lax.ppermute(values, 'head', pairs)  87.9 us
    reduce_scatter x1, waiting for transfers between devices, on_device(): lax.psum_scatter(joined.reshape(-1, lanes), 'dp', scatter_dimension=0, ti...  53.6 us
    convert_element_type x2, other arithmetic, chunk_pass(): hidden = activated.astype(jnp.bfloat16)  29.8 us
    add x1, other arithmetic, chunk_pass(): block_grad[:, :, :head_size, :head_size]  27.8 us
    unnamed x210, local copies, waits for them, and re-layouts  21.7 us
    dot_general x4, matrix products, trend_back(): return jnp.einsum('wts,wtd->wsd', rows, grads, precision=highest)  21.3 us
    ppermute x16, starting transfers between devices, swap(): return lax.ppermute(values, 'head', pairs)  19.6 us
  transfers between devices with their start and end apart: 17, of which 10 were waited for; matrix products, arithmetic and copies ran while one was open for 41% of the time, Pallas kernels for 0%

profile of v2, /device:TPU:0, one launch (start us, length us, event | category | flops | bytes accessed | tf_op | source)
XLA Modules:
  0.0 553.2 jit_solution(11069324397338331319)
XLA Ops:
  7.3 3.4 fusion.396
  10.7 3.0 collective-permute-start
  13.9 5.1 fusion.405
  21.1 4.2 fusion.407
  25.5 5.2 fusion.194
  30.7 4.8 fusion.192
  36.3 2.8 fusion.248
  40.3 3.2 convert_element_type.200
  43.5 2.8 fusion.246
  46.3 4.0 slice_negate_fusion
  50.3 2.4 fusion.62
  52.7 2.4 copy.134
  55.1 3.5 fusion.51
  58.5 3.3 fusion.50
  61.9 2.4 fusion.63
  66.6 2.5 fusion.53
  69.1 2.6 fusion.52
  72.7 2.8 fusion.60
  75.5 3.0 fusion.61
  87.5 14.7 %collective-permute-done.1 = bf16[16,96,256]{2,1,0:T(8,128)(2,1)S(1)} collective-permute-done((bf16[16,96,256]{2,1,0:T(8,128)(2,1)S(1)}, bf16[16,96,256]{2,1,0:T(8,128)(2,1)S(1)}, u32[]{:S(2)}, u32[]{:S(2)}) %collective-permute-start.1) | collective-permute-done | bytes 786464 | tf_op jit(solution)/shard_map/ppermute | solution.py:110
  102.2 3.5 fusion.404
  107.7 11.3 %collective-permute-done.5 = bf16[16,96,256]{2,1,0:T(8,128)(2,1)S(1)} collective-permute-done((bf16[16,96,256]{2,1,0:T(8,128)(2,1)S(1)}, bf16[16,96,256]{2,1,0:T(8,128)(2,1)S(1)}, u32[]{:S(2)}, u32[]{:S(2)}) %collective-permute-start.5) | collective-permute-done | bytes 786464 | tf_op jit(solution)/shard_map/ppermute | solution.py:110
  119.0 3.7 fusion.403
  124.8 2.6 fusion.206
  128.4 7.5 %collective-permute-done.2 = bf16[16,96,256]{2,1,0:T(8,128)(2,1)S(1)} collective-permute-done((bf16[16,96,256]{2,1,0:T(8,128)(2,1)S(1)}, bf16[16,96,256]{2,1,0:T(8,128)(2,1)S(1)}, u32[]{:S(2)}, u32[]{:S(2)}) %collective-permute-start.2) | collective-permute-done | bytes 786464 | tf_op jit(solution)/shard_map/ppermute | solution.py:110
  135.9 2.8 fusion.14
  138.8 14.9 %multiply_convert_fusion.1 = (bf16[16,96,1024]{2,1,0:T(8,128)(2,1)S(1)}, f32[16,96,1024]{2,1,0:T(8,128)}) fusion(f32[16,96,1024]{2,1,0:T(8,128)S(1)} %get-tuple-element.111, u16[96,1024]{1,0:T(8,128)(2,1)S(1)} %get-tuple-element.52, u16[96,1024]{1,0:T(8,128)(2,1)S(1)} %get-tuple-element.51), kind=kLoop, calls=%fused_computation.35 | loop fusion | flops 110100480 | bytes 16121856 | tf_op jit(solution)/shard_map/convert_element_type | solution.py:189
  153.7 7.5 %add_convert_fusion.1 = bf16[16,96,1024]{2,1,0:T(8,128)(2,1)S(1)} fusion(f32[16,96,1024]{2,1,0:T(8,128)} %get-tuple-element.69, f32[16,96,1024]{2,1,0:T(8,128)S(1)} %bitcast.353, f32[16,96,1024]{2,1,0:T(8,128)} %copy-done.23, bf16[16,96,256]{2,1,0:T(8,128)(2,1)} %collective-permute-done.8, bf16[1024,512]{1,0:T(8,128)(2,1)S(1)} %copy-done.11, s32[]{:T(128)S(6)} %select_n.165), kind=kOutput, calls=%fused_computation.21 | convolution fusion | flops 828899328 | bytes 23330820 | tf_op jit(solution)/shard_map/wtd,fd->wtf/dot_general | solution.py:44
  165.2 4.0 fusion.15
  169.3 14.9 %multiply_convert_fusion = (bf16[16,96,1024]{2,1,0:T(8,128)(2,1)S(1)}, f32[16,96,1024]{2,1,0:T(8,128)}) fusion(f32[16,96,1024]{2,1,0:T(8,128)S(1)} %get-tuple-element.108, u16[96,1024]{1,0:T(8,128)(2,1)S(1)} %get-tuple-element.54, u16[96,1024]{1,0:T(8,128)(2,1)S(1)} %get-tuple-element.53), kind=kLoop, calls=%fused_computation.22 | loop fusion | flops 110100480 | bytes 16121856 | tf_op jit(solution)/shard_map/convert_element_type | solution.py:189
  185.5 7.8 %add_convert_fusion = bf16[16,96,1024]{2,1,0:T(8,128)(2,1)} fusion(f32[16,96,1024]{2,1,0:T(8,128)} %get-tuple-element.71, f32[16,96,1024]{2,1,0:T(8,128)S(1)} %bitcast.351, f32[16,96,1024]{2,1,0:T(8,128)} %copy-done.22, bf16[16,96,256]{2,1,0:T(8,128)(2,1)} %collective-permute-done.12, bf16[1024,512]{1,0:T(8,128)(2,1)S(1)} %copy-done.11, s32[]{:T(128)S(6)} %select_n.165), kind=kOutput, calls=%fused_computation.20 | convolution fusion | flops 828899328 | bytes 23330820 | tf_op jit(solution)/shard_map/wtd,fd->wtf/dot_general | solution.py:44
  193.3 4.0 convolution_convert_fusion.4
  218.7 2.8 reshape_reshape.7
  221.4 4.1 add.318
  225.6 6.5 %copy.192 = f32[16,1024,32]{2,1,0:T(8,128)} copy(f32[16,1024,32]{1,2,0:T(8,128)} %bitcast.349) | data formatting | bytes 4194304 | tf_op jit(solution)/shard_map/transpose | solution.py:283
  232.0 7.0 %reshape.190 = f32[16,32768]{1,0:T(8,128)} reshape(f32[16,1024,32]{2,1,0:T(8,128)} %copy.192) | data formatting | bytes 4194304 | tf_op jit(solution)/shard_map/reshape | solution.py:283
  239.1 6.2 %fusion.408 = (bf16[16,96,256]{2,1,0:T(8,128)(2,1)S(1)}, f32[16,96,256]{2,1,0:T(8,128)}) fusion(f32[96,96]{1,0:T(8,128)S(1)} %copy-done.75, f32[96,96]{1,0:T(8,128)S(1)} %copy-done.77, f32[96,96]{1,0:T(8,128)} %constant.206, f32[96,96]{1,0:T(8,128)} %constant.204, f32[96,96]{1,0:T(8,128)} %constant.202, pred[32,96]{1,0:T(8,128)(4,1)S(1)} %get-tuple-element.98, ...), kind=kOutput, calls=%fused_computation.532 | convolution fusion | flops 456425472 | bytes 6491136 | tf_op jit(solution)/shard_map/wts,wtd->wsd/dot_general | solution.py:59
  248.8 5.8 %fusion.406 = (bf16[16,96,256]{2,1,0:T(8,128)(2,1)}, f32[16,96,256]{2,1,0:T(8,128)}) fusion(f32[96,96]{1,0:T(8,128)S(1)} %copy-done.75, f32[96,96]{1,0:T(8,128)S(1)} %copy-done.77, f32[96,96]{1,0:T(8,128)S(1)} %copy-done.81, f32[96,96]{1,0:T(8,128)S(1)} %copy-done.85, f32[96,96]{1,0:T(8,128)S(1)} %copy-done.89, pred[32,96]{1,0:T(8,128)(4,1)S(1)} %get-tuple-element.98, ...), kind=kOutput, calls=%fused_computation.530 | convolution fusion | flops 456425472 | bytes 6491136 | tf_op jit(solution)/shard_map/wts,wtd->wsd/dot_general | solution.py:59
  255.4 2.4 fusion.67
  258.2 2.7 fusion.232
  260.9 4.9 collective-permute-done.10
  270.1 3.4 fusion.55
  273.5 3.4 fusion.54
  277.3 2.4 add_convert_fusion.6
  279.8 2.6 copy.165
  282.4 2.6 fusion.57
  285.0 2.4 fusion.56
  287.8 6.3 %fusion.59 = bf16[16,4,48,128]{3,0,2,1:T(8,128)(2,1)} fusion(bf16[16,4,48,128]{3,2,0,1:T(8,128)(2,1)S(1)} %pad_maximum_fusion.5, bf16[4,48,64,64]{3,2,1,0:T(8,128)(2,1)} %get-tuple-element.79, bf16[4,48,64,64]{3,2,1,0:T(8,128)(2,1)S(1)} %copy-done.36, bf16[4,48,64,128]{3,2,1,0:T(8,128)(2,1)S(1)} %bitcast.325), kind=kOutput, calls=%fused_computation.150 | convolution fusion | flops 119930880 | bytes 7864320 | tf_op jit(solution)/shard_map/whmo,hmio->whmi/dot_general | solution.py:44
  294.2 5.6 %fusion.176 = f32[4,48,128,128]{3,2,1,0:T(8,128)} fusion(bf16[16,4,48,128]{3,2,0,1:T(8,128)(2,1)S(1)} %pad_maximum_fusion.5, bf16[16,4,48,128]{3,2,0,1:T(8,128)(2,1)S(1)} %copy-done.30), kind=kOutput, calls=%fused_computation.279 | convolution fusion | flops 100663296 | bytes 14155776 | tf_op jit(solution)/shard_map/whmi,whmo->hmio/dot_general | solution.py:44
  300.3 6.3 %fusion.58 = bf16[16,4,48,128]{3,0,2,1:T(8,128)(2,1)S(1)} fusion(bf16[16,4,48,128]{3,2,0,1:T(8,128)(2,1)S(1)} %pad_maximum_fusion.4, bf16[4,48,64,64]{3,2,1,0:T(8,128)(2,1)} %get-tuple-element.79, bf16[4,48,64,64]{3,2,1,0:T(8,128)(2,1)} %get-tuple-element.78, bf16[4,48,64,128]{3,2,1,0:T(8,128)(2,1)S(1)} %bitcast.326), kind=kOutput, calls=%fused_computation.149 | convolution fusion | flops 119930880 | bytes 7864320 | tf_op jit(solution)/shard_map/whmo,hmio->whmi/dot_general | solution.py:44
  306.6 5.8 %fusion.179 = f32[4,48,128,128]{3,2,1,0:T(8,128)} fusion(bf16[16,4,48,128]{3,2,0,1:T(8,128)(2,1)S(1)} %pad_maximum_fusion.4, bf16[16,4,48,128]{3,2,0,1:T(8,128)(2,1)S(1)} %copy-done.28), kind=kOutput, calls=%fused_computation.282 | convolution fusion | flops 100663296 | bytes 14155776 | tf_op jit(solution)/shard_map/whmi,whmo->hmio/dot_general | solution.py:44
  322.3 2.4 fusion.64
  324.7 2.4 fusion.66
  340.9 27.8 %slice_add_fusion = (f32[4,48,64,64]{3,2,1,0:T(8,128)}, f32[4,48,64,64]{3,2,1,0:T(8,128)}, f32[4,48,64,64]{3,2,1,0:T(8,128)}, f32[4,48,64,64]{3,2,1,0:T(8,128)}) fusion(f32[4,48,128,128]{3,2,1,0:T(8,128)} %fusion.179, f32[4,48,128,128]{3,2,1,0:T(8,128)} %fusion.176), kind=kLoop, calls=%fused_computation.15 | loop fusion | flops 3145728 | bytes 37748736 | tf_op jit(solution)/shard_map/add | solution.py:249
  368.8 10.2 %maximum_add_fusion = f32[4,48,64,128]{3,2,1,0:T(8,128)S(1)} fusion(f32[4,48,64,64]{3,2,1,0:T(8,128)} %get-tuple-element.120, f32[4,48,64,64]{3,2,1,0:T(8,128)} %get-tuple-element.121, f32[4,48,64,64]{3,2,1,0:T(8,128)} %get-tuple-element.73, f32[4,48,64,64]{3,2,1,0:T(8,128)} %get-tuple-element.72), kind=kLoop, calls=%fused_computation.19 | loop fusion | flops 4718592 | bytes 18874368 | tf_op jit(solution)/shard_map/add | solution.py:272
  379.4 6.3 %bitcast_dynamic-update-slice_fusion = f32[16,180224]{1,0:T(8,128)} fusion(f32[16,180224]{1,0:T(8,128)} %constant_dynamic-update-slice_fusion.3, f32[2,8,768,128]{3,2,1,0:T(8,128)S(1)} %bitcast.343), kind=kLoop, calls=%fused_computation.13 | loop fusion | bytes 12582912
  389.5 12.1 %reshape.191 = f32[22528,128]{1,0:T(8,128)} reshape(f32[16,180224]{1,0:T(8,128)} %constant_dynamic-update-slice_fusion) | data formatting | bytes 23068672 | tf_op jit(solution)/shard_map/reshape | solution.py:295
  406.3 3.0 convolution_convert_fusion.10
  414.6 15.2 %collective-permute-done.3 = bf16[16,96,256]{2,1,0:T(8,128)(2,1)S(1)} collective-permute-done((bf16[16,96,256]{2,1,0:T(8,128)(2,1)S(1)}, bf16[16,96,256]{2,1,0:T(8,128)(2,1)S(1)}, u32[]{:S(2)}, u32[]{:S(2)}) %collective-permute-start.3) | collective-permute-done | bytes 786464 | tf_op jit(solution)/shard_map/ppermute | solution.py:110
  435.4 11.2 %collective-permute-done.7 = bf16[16,96,256]{2,1,0:T(8,128)(2,1)S(1)} collective-permute-done((bf16[16,96,256]{2,1,0:T(8,128)(2,1)S(1)}, bf16[16,96,256]{2,1,0:T(8,128)(2,1)S(1)}, u32[]{:S(2)}, u32[]{:S(2)}) %collective-permute-start.7) | collective-permute-done | bytes 786464 | tf_op jit(solution)/shard_map/ppermute | solution.py:110
  446.6 2.4 convolution_subtract_fusion.4
  450.9 12.6 %collective-permute-done.11 = bf16[16,96,256]{2,1,0:T(8,128)(2,1)S(1)} collective-permute-done((bf16[16,96,256]{2,1,0:T(8,128)(2,1)S(1)}, bf16[16,96,256]{2,1,0:T(8,128)(2,1)S(1)}, u32[]{:S(2)}, u32[]{:S(2)}) %collective-permute-start.11) | collective-permute-done | bytes 786464 | tf_op jit(solution)/shard_map/ppermute | solution.py:110
  464.0 10.1 %collective-permute-done.15 = bf16[16,96,256]{2,1,0:T(8,128)(2,1)S(1)} collective-permute-done((bf16[16,96,256]{2,1,0:T(8,128)(2,1)S(1)}, bf16[16,96,256]{2,1,0:T(8,128)(2,1)S(1)}, u32[]{:S(2)}, u32[]{:S(2)}) %collective-permute-start.15) | collective-permute-done | bytes 786464 | tf_op jit(solution)/shard_map/ppermute | solution.py:110
  476.5 53.6 %reduce-scatter.2.cloned.1.call-done = f32[1408,128]{1,0:T(8,128)} async-done(((f32[22528,128]{1,0:T(8,128)}), f32[1408,128]{1,0:T(8,128)}) %reduce-scatter.2.cloned.1.call-update) | async-done | bytes 720912 | tf_op jit(solution)/shard_map/reduce_scatter | solution.py:294
  (334 shorter events, 121.9 us)
Async XLA Ops:
  7.2 522.9 %reduce-scatter.2.cloned.1.call-start = ((), (), s32[]{:S(2)}) async-start(), calls=%async_computation.1 | async-start | bytes 12255232 | tf_op jit(solution)/shard_map/reduce_scatter | solution.py:294
  10.7 39.6 %collective-permute-start = (bf16[16,96,256]{2,1,0:T(8,128)(2,1)}, bf16[16,96,256]{2,1,0:T(8,128)(2,1)}, u32[]{:S(2)}, u32[]{:S(2)}) collective-permute-start(bf16[16,96,256]{2,1,0:T(8,128)(2,1)} %get-tuple-element.76), channel_id=1, source_target_pairs={{0,1},{1,0},{2,3},{3,2},{4,5},{5,4},{6,7},{7,6},{8,9},{9,8},{10,11... | collective-permute-start | bytes 2359304 | tf_op jit(solution)/shard_map/ppermute | solution.py:110
  13.7 48.2 %collective-permute-start.4 = (bf16[16,96,256]{2,1,0:T(8,128)(2,1)}, bf16[16,96,256]{2,1,0:T(8,128)(2,1)}, u32[]{:S(2)}, u32[]{:S(2)}) collective-permute-start(bf16[16,96,256]{2,1,0:T(8,128)(2,1)} %get-tuple-element.77), channel_id=1, source_target_pairs={{0,1},{1,0},{2,3},{3,2},{4,5},{5,4},{6,7},{7,6},{8,9},{9,8},{10,11... | collective-permute-start | bytes 2359304 | tf_op jit(solution)/shard_map/ppermute | solution.py:110
  13.7 7.3 %copy-start.61 = (pred[32,96]{1,0:T(8,128)(4,1)}, pred[32,96]{1,0:T(8,128)(4,1)S(1)}, u32[]{:S(2)}) copy-start(pred[32,96]{1,0:T(8,128)(4,1)S(1)} %get-tuple-element.94) | copy-start | bytes 9220
  13.8 7.3 %copy-start.63 = (pred[32,96]{1,0:T(8,128)(4,1)}, pred[32,96]{1,0:T(8,128)(4,1)S(1)}, u32[]{:S(2)}) copy-start(pred[32,96]{1,0:T(8,128)(4,1)S(1)} %get-tuple-element.99) | copy-start | bytes 9220
  13.8 7.2 %copy-start.65 = (pred[32,96]{1,0:T(8,128)(4,1)}, pred[32,96]{1,0:T(8,128)(4,1)S(1)}, u32[]{:S(2)}) copy-start(pred[32,96]{1,0:T(8,128)(4,1)S(1)} %get-tuple-element.100) | copy-start | bytes 9220
  13.8 7.2 %copy-start.67 = (pred[32,96]{1,0:T(8,128)(4,1)}, pred[32,96]{1,0:T(8,128)(4,1)S(1)}, u32[]{:S(2)}) copy-start(pred[32,96]{1,0:T(8,128)(4,1)S(1)} %get-tuple-element.101) | copy-start | bytes 9220
  13.8 7.2 %copy-start.69 = (pred[32,96]{1,0:T(8,128)(4,1)}, pred[32,96]{1,0:T(8,128)(4,1)S(1)}, u32[]{:S(2)}) copy-start(pred[32,96]{1,0:T(8,128)(4,1)S(1)} %get-tuple-element.102) | copy-start | bytes 9220
  19.0 166.4 %collective-permute-start.12 = (bf16[16,96,256]{2,1,0:T(8,128)(2,1)}, bf16[16,96,256]{2,1,0:T(8,128)(2,1)}, u32[]{:S(2)}, u32[]{:S(2)}) collective-permute-start(bf16[16,96,256]{2,1,0:T(8,128)(2,1)} %get-tuple-element.112), channel_id=1, source_target_pairs={{0,1},{1,0},{2,3},{3,2},{4,5},{5,4},{6,7},{7,6},{8,9},{9,8},{10,11... | collective-permute-start | bytes 2359304 | tf_op jit(solution)/shard_map/ppermute | solution.py:110
  25.3 128.4 %collective-permute-start.8 = (bf16[16,96,256]{2,1,0:T(8,128)(2,1)}, bf16[16,96,256]{2,1,0:T(8,128)(2,1)}, u32[]{:S(2)}, u32[]{:S(2)}) collective-permute-start(bf16[16,96,256]{2,1,0:T(8,128)(2,1)} %get-tuple-element.116), channel_id=1, source_target_pairs={{0,1},{1,0},{2,3},{3,2},{4,5},{5,4},{6,7},{7,6},{8,9},{9,8},{10,11... | collective-permute-start | bytes 2359304 | tf_op jit(solution)/shard_map/ppermute | solution.py:110
  81.7 20.5 %collective-permute-start.1 = (bf16[16,96,256]{2,1,0:T(8,128)(2,1)S(1)}, bf16[16,96,256]{2,1,0:T(8,128)(2,1)S(1)}, u32[]{:S(2)}, u32[]{:S(2)}) collective-permute-start(bf16[16,96,256]{2,1,0:T(8,128)(2,1)S(1)} %convolution_convert_fusion.11), channel_id=1, source_target_pairs={{0,1},{1,0},{2,3},{3,2},{4,5},{5,4},{6,7},{7,6},{8,9},{9,8},{10,11... | collective-permute-start | bytes 2359304 | tf_op jit(solution)/shard_map/ppermute | solution.py:110
  86.3 15.9 %copy-start.51 = (f32[32,96,256]{2,1,0:T(8,128)S(1)}, f32[32,96,256]{2,1,0:T(8,128)}, u32[]{:S(2)}) copy-start(f32[32,96,256]{2,1,0:T(8,128)} %param.20) | copy-start | bytes 9437188
  86.3 15.9 %copy-start.80 = (f32[96,96]{1,0:T(8,128)S(1)}, f32[96,96]{1,0:T(8,128)}, u32[]{:S(2)}) copy-start(f32[96,96]{1,0:T(8,128)} %constant.206) | copy-start | bytes 110596
  86.3 15.9 %copy-start.84 = (f32[96,96]{1,0:T(8,128)S(1)}, f32[96,96]{1,0:T(8,128)}, u32[]{:S(2)}) copy-start(f32[96,96]{1,0:T(8,128)} %constant.204) | copy-start | bytes 110596
  86.4 15.8 %copy-start.88 = (f32[96,96]{1,0:T(8,128)S(1)}, f32[96,96]{1,0:T(8,128)}, u32[]{:S(2)}) copy-start(f32[96,96]{1,0:T(8,128)} %constant.202) | copy-start | bytes 110596
  86.4 32.7 %collective-permute-start.5 = (bf16[16,96,256]{2,1,0:T(8,128)(2,1)S(1)}, bf16[16,96,256]{2,1,0:T(8,128)(2,1)S(1)}, u32[]{:S(2)}, u32[]{:S(2)}) collective-permute-start(bf16[16,96,256]{2,1,0:T(8,128)(2,1)S(1)} %convolution_convert_fusion.9), channel_id=1, source_target_pairs={{0,1},{1,0},{2,3},{3,2},{4,5},{5,4},{6,7},{7,6},{8,9},{9,8},{10,11... | collective-permute-start | bytes 2359304 | tf_op jit(solution)/shard_map/ppermute | solution.py:110
  105.7 19.1 %copy-start.13 = (bf16[512,1024]{1,0:T(8,128)(2,1)S(1)}, bf16[512,1024]{1,0:T(8,128)(2,1)}, u32[]{:S(2)}) copy-start(bf16[512,1024]{1,0:T(8,128)(2,1)} %convert_element_type.220) | copy-start | bytes 3145732
  105.7 30.2 %collective-permute-start.2 = (bf16[16,96,256]{2,1,0:T(8,128)(2,1)S(1)}, bf16[16,96,256]{2,1,0:T(8,128)(2,1)S(1)}, u32[]{:S(2)}, u32[]{:S(2)}) collective-permute-start(bf16[16,96,256]{2,1,0:T(8,128)(2,1)S(1)} %get-tuple-element.109), channel_id=1, source_target_pairs={{0,1},{1,0},{2,3},{3,2},{4,5},{5,4},{6,7},{7,6},{8,9},{9,8},{10,11... | collective-permute-start | bytes 2359304 | tf_op jit(solution)/shard_map/ppermute | solution.py:110
  122.8 42.4 %collective-permute-start.6 = (bf16[16,96,256]{2,1,0:T(8,128)(2,1)}, bf16[16,96,256]{2,1,0:T(8,128)(2,1)}, u32[]{:S(2)}, u32[]{:S(2)}) collective-permute-start(bf16[16,96,256]{2,1,0:T(8,128)(2,1)} %get-tuple-element.106), channel_id=1, source_target_pairs={{0,1},{1,0},{2,3},{3,2},{4,5},{5,4},{6,7},{7,6},{8,9},{9,8},{10,11... | collective-permute-start | bytes 2359304 | tf_op jit(solution)/shard_map/ppermute | solution.py:110
  127.4 26.3 %slice-start.2 = ((s8[6291456]{0:T(1024)(128)(4,1)}), s8[4194304]{0:T(1024)(128)(4,1)S(1)}, s32[]{:S(2)}) async-start(s8[6291456]{0:T(1024)(128)(4,1)} %bitcast.352), calls=%async_computation.4 | async-start | bytes 8388608
  128.4 25.3 %slice-start.3 = ((s8[6291456]{0:T(1024)(128)(4,1)}), s8[2097152]{0:T(1024)(128)(4,1)S(1)}, s32[]{:S(2)}) async-start(s8[6291456]{0:T(1024)(128)(4,1)} %bitcast.352), calls=%async_computation.5 | async-start | bytes 4194304
  138.8 14.9 %copy-start.23 = (f32[16,96,1024]{2,1,0:T(8,128)}, f32[16,96,1024]{2,1,0:T(8,128)S(1)}, u32[]{:S(2)}) copy-start(f32[16,96,1024]{2,1,0:T(8,128)S(1)} %get-tuple-element.111) | copy-start | bytes 18874372
  138.8 14.9 %copy-start.11 = (bf16[1024,512]{1,0:T(8,128)(2,1)S(1)}, bf16[1024,512]{1,0:T(8,128)(2,1)}, u32[]{:S(2)}) copy-start(bf16[1024,512]{1,0:T(8,128)(2,1)} %copy-done.10) | copy-start | bytes 3145732
  153.7 50.9 %copy-start.6 = (bf16[16,96,1024]{2,1,0:T(8,128)(2,1)}, bf16[16,96,1024]{2,1,0:T(8,128)(2,1)S(1)}, u32[]{:S(2)}) copy-start(bf16[16,96,1024]{2,1,0:T(8,128)(2,1)S(1)} %get-tuple-element.68) | copy-start | bytes 9437188
  161.3 8.0 %copy-start.38 = (bf16[16,96,1024]{2,1,0:T(8,128)(2,1)}, bf16[16,96,1024]{2,1,0:T(8,128)(2,1)S(1)}, u32[]{:S(2)}) copy-start(bf16[16,96,1024]{2,1,0:T(8,128)(2,1)S(1)} %add_convert_fusion.1) | copy-start | bytes 9437188
  163.2 75.8 %collective-permute-start.9 = (bf16[16,96,256]{2,1,0:T(8,128)(2,1)}, bf16[16,96,256]{2,1,0:T(8,128)(2,1)}, u32[]{:S(2)}, u32[]{:S(2)}) collective-permute-start(bf16[16,96,256]{2,1,0:T(8,128)(2,1)} %convolution_convert_fusion.7), channel_id=1, source_target_pairs={{0,1},{1,0},{2,3},{3,2},{4,5},{5,4},{6,7},{7,6},{8,9},{9,8},{10,11... | collective-permute-start | bytes 2359304 | tf_op jit(solution)/shard_map/ppermute | solution.py:110
  165.2 20.2 %slice-start = ((s8[6291456]{0:T(1024)(128)(4,1)}), s8[4194304]{0:T(1024)(128)(4,1)S(1)}, s32[]{:S(2)}) async-start(s8[6291456]{0:T(1024)(128)(4,1)} %bitcast.350), calls=%async_computation.2 | async-start | bytes 8388608
  169.2 14.9 %copy-start.22 = (f32[16,96,1024]{2,1,0:T(8,128)}, f32[16,96,1024]{2,1,0:T(8,128)S(1)}, u32[]{:S(2)}) copy-start(f32[16,96,1024]{2,1,0:T(8,128)S(1)} %get-tuple-element.108) | copy-start | bytes 18874372
  169.3 15.2 %copy-start.39 = (bf16[16,96,1024]{2,1,0:T(8,128)(2,1)S(1)}, bf16[16,96,1024]{2,1,0:T(8,128)(2,1)}, u32[]{:S(2)}) copy-start(bf16[16,96,1024]{2,1,0:T(8,128)(2,1)} %copy-done.38) | copy-start | bytes 9437188
  169.3 16.2 %slice-start.1 = ((s8[6291456]{0:T(1024)(128)(4,1)}), s8[2097152]{0:T(1024)(128)(4,1)S(1)}, s32[]{:S(2)}) async-start(s8[6291456]{0:T(1024)(128)(4,1)} %bitcast.350), calls=%async_computation.3 | async-start | bytes 4194304
  184.2 23.7 %copy-start.8 = (bf16[16,96,1024]{2,1,0:T(8,128)(2,1)}, bf16[16,96,1024]{2,1,0:T(8,128)(2,1)S(1)}, u32[]{:S(2)}) copy-start(bf16[16,96,1024]{2,1,0:T(8,128)(2,1)S(1)} %get-tuple-element.70) | copy-start | bytes 9437188
  199.7 48.3 %collective-permute-start.13 = (bf16[16,96,256]{2,1,0:T(8,128)(2,1)}, bf16[16,96,256]{2,1,0:T(8,128)(2,1)}, u32[]{:S(2)}, u32[]{:S(2)}) collective-permute-start(bf16[16,96,256]{2,1,0:T(8,128)(2,1)} %convolution_convert_fusion.4), channel_id=1, source_target_pairs={{0,1},{1,0},{2,3},{3,2},{4,5},{5,4},{6,7},{7,6},{8,9},{9,8},{10,11... | collective-permute-start | bytes 2359304 | tf_op jit(solution)/shard_map/ppermute | solution.py:110
  239.0 8.3 %copy-start.1 = (bf16[16,96,4,64]{1,3,2,0:T(8,128)(2,1)S(1)}, bf16[16,96,4,64]{1,3,2,0:T(8,128)(2,1)}, u32[]{:S(2)}) copy-start(bf16[16,96,4,64]{1,3,2,0:T(8,128)(2,1)} %copy-done) | copy-start | bytes 2359300
  239.0 9.7 %copy-start.48 = (f32[16,96,256]{2,1,0:T(8,128)S(1)}, f32[16,96,256]{2,1,0:T(8,128)}, u32[]{:S(2)}) copy-start(f32[16,96,256]{2,1,0:T(8,128)} %fusion.202) | copy-start | bytes 4718596
  239.0 9.7 %copy-start.81 = (f32[96,96]{1,0:T(8,128)S(1)}, f32[96,96]{1,0:T(8,128)}, u32[]{:S(2)}) copy-start(f32[96,96]{1,0:T(8,128)} %constant.206) | copy-start | bytes 110596
  239.1 9.7 %copy-start.85 = (f32[96,96]{1,0:T(8,128)S(1)}, f32[96,96]{1,0:T(8,128)}, u32[]{:S(2)}) copy-start(f32[96,96]{1,0:T(8,128)} %constant.204) | copy-start | bytes 110596
  239.1 9.7 %copy-start.89 = (f32[96,96]{1,0:T(8,128)S(1)}, f32[96,96]{1,0:T(8,128)}, u32[]{:S(2)}) copy-start(f32[96,96]{1,0:T(8,128)} %constant.202) | copy-start | bytes 110596
  239.1 9.7 %copy-start.91 = (f32[16,96,256]{2,1,0:T(8,128)S(1)}, f32[16,96,256]{2,1,0:T(8,128)}, u32[]{:S(2)}) copy-start(f32[16,96,256]{2,1,0:T(8,128)} %get-tuple-element.113) | copy-start | bytes 4718596
  245.3 20.4 %collective-permute-start.10 = (bf16[16,96,256]{2,1,0:T(8,128)(2,1)S(1)}, bf16[16,96,256]{2,1,0:T(8,128)(2,1)S(1)}, u32[]{:S(2)}, u32[]{:S(2)}) collective-permute-start(bf16[16,96,256]{2,1,0:T(8,128)(2,1)S(1)} %get-tuple-element.118), channel_id=1, source_target_pairs={{0,1},{1,0},{2,3},{3,2},{4,5},{5,4},{6,7},{7,6},{8,9},{9,8},{10,11... | collective-permute-start | bytes 2359304 | tf_op jit(solution)/shard_map/ppermute | solution.py:110
  254.5 22.8 %collective-permute-start.14 = (bf16[16,96,256]{2,1,0:T(8,128)(2,1)}, bf16[16,96,256]{2,1,0:T(8,128)(2,1)}, u32[]{:S(2)}, u32[]{:S(2)}) collective-permute-start(bf16[16,96,256]{2,1,0:T(8,128)(2,1)} %get-tuple-element.114), channel_id=1, source_target_pairs={{0,1},{1,0},{2,3},{3,2},{4,5},{5,4},{6,7},{7,6},{8,9},{9,8},{10,11... | collective-permute-start | bytes 2359304 | tf_op jit(solution)/shard_map/ppermute | solution.py:110
  270.1 7.2 %copy-start.26 = (f32[16,96,256]{2,1,0:T(8,128)S(1)}, f32[16,96,256]{2,1,0:T(8,128)}, u32[]{:S(2)}) copy-start(f32[16,96,256]{2,1,0:T(8,128)} %fusion.232) | copy-start | bytes 4718596
  314.7 7.6 %copy-start.2 = (bf16[16,96,4,64]{1,3,2,0:T(8,128)(2,1)S(1)}, bf16[16,96,4,64]{1,3,2,0:T(8,128)(2,1)}, u32[]{:S(2)}) copy-start(bf16[16,96,4,64]{1,3,2,0:T(8,128)(2,1)} %copy-done) | copy-start | bytes 2359300
  317.1 7.6 %copy-start.5 = (bf16[16,96,4,64]{1,3,2,0:T(8,128)(2,1)S(1)}, bf16[16,96,4,64]{1,3,2,0:T(8,128)(2,1)}, u32[]{:S(2)}) copy-start(bf16[16,96,4,64]{1,3,2,0:T(8,128)(2,1)} %copy-done.3) | copy-start | bytes 2359300
  409.3 20.5 %collective-permute-start.3 = (bf16[16,96,256]{2,1,0:T(8,128)(2,1)S(1)}, bf16[16,96,256]{2,1,0:T(8,128)(2,1)S(1)}, u32[]{:S(2)}, u32[]{:S(2)}) collective-permute-start(bf16[16,96,256]{2,1,0:T(8,128)(2,1)S(1)} %convolution_convert_fusion.10), channel_id=1, source_target_pairs={{0,1},{1,0},{2,3},{3,2},{4,5},{5,4},{6,7},{7,6},{8,9},{9,8},{10,11... | collective-permute-start | bytes 2359304 | tf_op jit(solution)/shard_map/ppermute | solution.py:110
  411.9 34.7 %collective-permute-start.7 = (bf16[16,96,256]{2,1,0:T(8,128)(2,1)S(1)}, bf16[16,96,256]{2,1,0:T(8,128)(2,1)S(1)}, u32[]{:S(2)}, u32[]{:S(2)}) collective-permute-start(bf16[16,96,256]{2,1,0:T(8,128)(2,1)S(1)} %convolution_convert_fusion.8), channel_id=1, source_target_pairs={{0,1},{1,0},{2,3},{3,2},{4,5},{5,4},{6,7},{7,6},{8,9},{9,8},{10,11... | collective-permute-start | bytes 2359304 | tf_op jit(solution)/shard_map/ppermute | solution.py:110
  413.5 16.3 %copy-start.62 = (pred[32,96]{1,0:T(8,128)(4,1)S(1)}, pred[32,96]{1,0:T(8,128)(4,1)}, u32[]{:S(2)}) copy-start(pred[32,96]{1,0:T(8,128)(4,1)} %copy-done.61) | copy-start | bytes 9220
  413.5 16.3 %copy-start.64 = (pred[32,96]{1,0:T(8,128)(4,1)S(1)}, pred[32,96]{1,0:T(8,128)(4,1)}, u32[]{:S(2)}) copy-start(pred[32,96]{1,0:T(8,128)(4,1)} %copy-done.63) | copy-start | bytes 9220
  413.5 16.3 %copy-start.66 = (pred[32,96]{1,0:T(8,128)(4,1)S(1)}, pred[32,96]{1,0:T(8,128)(4,1)}, u32[]{:S(2)}) copy-start(pred[32,96]{1,0:T(8,128)(4,1)} %copy-done.65) | copy-start | bytes 9220
  413.5 16.3 %copy-start.68 = (pred[32,96]{1,0:T(8,128)(4,1)S(1)}, pred[32,96]{1,0:T(8,128)(4,1)}, u32[]{:S(2)}) copy-start(pred[32,96]{1,0:T(8,128)(4,1)} %copy-done.67) | copy-start | bytes 9220
  413.5 16.3 %copy-start.70 = (pred[32,96]{1,0:T(8,128)(4,1)S(1)}, pred[32,96]{1,0:T(8,128)(4,1)}, u32[]{:S(2)}) copy-start(pred[32,96]{1,0:T(8,128)(4,1)} %copy-done.69) | copy-start | bytes 9220
  413.5 16.3 %copy-start.76 = (f32[96,96]{1,0:T(8,128)S(1)}, f32[96,96]{1,0:T(8,128)}, u32[]{:S(2)}) copy-start(f32[96,96]{1,0:T(8,128)} %constant.210) | copy-start | bytes 110596
  413.6 16.3 %copy-start.78 = (f32[96,96]{1,0:T(8,128)S(1)}, f32[96,96]{1,0:T(8,128)}, u32[]{:S(2)}) copy-start(f32[96,96]{1,0:T(8,128)} %constant.208) | copy-start | bytes 110596
  413.6 16.3 %copy-start.82 = (f32[96,96]{1,0:T(8,128)S(1)}, f32[96,96]{1,0:T(8,128)}, u32[]{:S(2)}) copy-start(f32[96,96]{1,0:T(8,128)} %constant.206) | copy-start | bytes 110596
  413.6 16.3 %copy-start.86 = (f32[96,96]{1,0:T(8,128)S(1)}, f32[96,96]{1,0:T(8,128)}, u32[]{:S(2)}) copy-start(f32[96,96]{1,0:T(8,128)} %constant.204) | copy-start | bytes 110596
  413.6 16.3 %copy-start.90 = (f32[96,96]{1,0:T(8,128)S(1)}, f32[96,96]{1,0:T(8,128)}, u32[]{:S(2)}) copy-start(f32[96,96]{1,0:T(8,128)} %constant.202) | copy-start | bytes 110596
  413.6 16.3 %copy-start.93 = (f32[16,96,256]{2,1,0:T(8,128)S(1)}, f32[16,96,256]{2,1,0:T(8,128)}, u32[]{:S(2)}) copy-start(f32[16,96,256]{2,1,0:T(8,128)} %get-tuple-element.110) | copy-start | bytes 4718596
  432.2 14.4 %copy-start.92 = (f32[16,96,256]{2,1,0:T(8,128)S(1)}, f32[16,96,256]{2,1,0:T(8,128)}, u32[]{:S(2)}) copy-start(f32[16,96,256]{2,1,0:T(8,128)} %get-tuple-element.107) | copy-start | bytes 4718596
  432.8 30.7 %collective-permute-start.11 = (bf16[16,96,256]{2,1,0:T(8,128)(2,1)S(1)}, bf16[16,96,256]{2,1,0:T(8,128)(2,1)S(1)}, u32[]{:S(2)}, u32[]{:S(2)}) collective-permute-start(bf16[16,96,256]{2,1,0:T(8,128)(2,1)S(1)} %convolution_convert_fusion.5), channel_id=1, source_target_pairs={{0,1},{1,0},{2,3},{3,2},{4,5},{5,4},{6,7},{7,6},{8,9},{9,8},{10,11... | collective-permute-start | bytes 2359304 | tf_op jit(solution)/shard_map/ppermute | solution.py:110
  434.9 39.2 %collective-permute-start.15 = (bf16[16,96,256]{2,1,0:T(8,128)(2,1)S(1)}, bf16[16,96,256]{2,1,0:T(8,128)(2,1)S(1)}, u32[]{:S(2)}, u32[]{:S(2)}) collective-permute-start(bf16[16,96,256]{2,1,0:T(8,128)(2,1)S(1)} %convolution_convert_fusion.2), channel_id=1, source_target_pairs={{0,1},{1,0},{2,3},{3,2},{4,5},{5,4},{6,7},{7,6},{8,9},{9,8},{10,11... | collective-permute-start | bytes 2359304 | tf_op jit(solution)/shard_map/ppermute | solution.py:110
  449.0 14.5 %copy-start.46 = (f32[16,96,256]{2,1,0:T(8,128)S(1)}, f32[16,96,256]{2,1,0:T(8,128)}, u32[]{:S(2)}) copy-start(f32[16,96,256]{2,1,0:T(8,128)} %get-tuple-element.119) | copy-start | bytes 4718596
  450.9 23.2 %copy-start.47 = (f32[16,96,256]{2,1,0:T(8,128)S(1)}, f32[16,96,256]{2,1,0:T(8,128)}, u32[]{:S(2)}) copy-start(f32[16,96,256]{2,1,0:T(8,128)} %get-tuple-element.115) | copy-start | bytes 4718596
  476.5 60.1 %copy-start.44 = (f32[1024,32]{1,0:T(8,128)S(1)}, f32[1024,32]{1,0:T(8,128)}, u32[]{:S(2)}) copy-start(f32[1024,32]{1,0:T(8,128)} %copy.195) | copy-start | bytes 393220
  476.5 60.1 %copy-start.45 = (f32[1024,32]{1,0:T(8,128)S(1)}, f32[1024,32]{1,0:T(8,128)}, u32[]{:S(2)}) copy-start(f32[1024,32]{1,0:T(8,128)} %copy.196) | copy-start | bytes 393220
  536.6 7.2 %slice-start.4 = ((f32[1408,128]{1,0:T(8,128)}), f32[768,128]{1,0:T(8,128)S(1)}, s32[]{:S(2)}) async-start(f32[1408,128]{1,0:T(8,128)} %reduce-scatter.2.cloned.1.call-done), calls=%async_computation.6 | async-start | bytes 786432 | tf_op jit(solution)/shard_map/slice | solution.py:301
  (52 other events, 236.6 us)
Sparse Core Ops, SparseCore 0:
  401.8 128.2 reduce-scatter.1
